TPU v7x, 32 devices: a whole 2x2x4 slice. The times are simulated.
32 devices in a mesh: req: 4 (over z), ctx: 8 (over y, x, core).
Axes of the slice: x: 2, y: 2, z: 4, core: 2. Of those that a mesh axis runs over, the one named last changes fastest.
Arguments:
- hidden_in: bfloat16 [4096, 2048], P(('req', 'ctx')), may hold values from -3 to 3
- queries: bfloat16 [4096, 1024], P(('req', 'ctx')), may hold values from -10 to 10
- span_keys: bfloat16 [4096, 1024], P(('req', 'ctx')), may hold values from -10 to 10
- span_values: bfloat16 [4096, 1024], P(('req', 'ctx')), may hold values from -6 to 6
- cache_keys: bfloat16 [6144, 1024], P(('req', 'ctx')), may hold values from -6 to 6
- cache_values: bfloat16 [6144, 1024], P(('req', 'ctx')), may hold values from -6 to 6
- cache_lengths: int32 [4], replicated, may hold values from 0 to 1536, as said below
- slot_request: int32 [4], replicated, may hold values from 0 to 3, each once
- out_weight: bfloat16 [1024, 2048], replicated, may hold values from -1.5 to 1.5
- norm_gain: float32 [2048], replicated, may hold values from 0.1 to 1.9
- expert_ids: int32 [4096, 8], P(('req', 'ctx')), may hold values from 0 to 15, all different within a row; in each aligned block of 128 rows (0 to 127, 128 to 255, ...) at most 128 rows name the same one
- expert_gates: float32 [4096, 8], P(('req', 'ctx')), may hold values from 0.05 to 0.5
- gate_proj: bfloat16 [16, 2048, 512], P('ctx'), may hold values from -0.125 to 0.125
- up_proj: bfloat16 [16, 2048, 512], P('ctx'), may hold values from -0.125 to 0.125
- down_proj: bfloat16 [16, 512, 2048], P('ctx'), may hold values from -0.25 to 0.25
Outputs:
- layer_out: bfloat16 [4096, 2048], P(('req', 'ctx'))
Inputs may be any that keep to these rules, and one draw needn't show every extreme that they name: `cache_lengths`: some request has exactly 1536 cached positions.
All inputs are finite; a program needn't handle non-finite values.
Results may differ from a plain program's by a relative error of at most 0.015.
Values may be sent and summed in bfloat16 or wider, within the bound.
No kernel may reach another device: no remote copies, remote signals or barrier semaphores. Data moves between devices by JAX's collectives and lax.ppermute only.
A program may use at most 192 MiB of HBM per device.

v0:
```python
import itertools
import math

import jax
import jax.numpy as jnp
from jax import lax
from jax.sharding import PartitionSpec as P

HEAD_DIM = 128


def attend_gathered(queries, span_keys, span_values, cache_keys, cache_values, length):
    token_count, column_count = queries.shape
    head_count = column_count // HEAD_DIM
    cached_rows = cache_keys.shape[0]
    block_rows = token_count + cached_rows
    scaling = 1.0 / math.sqrt(HEAD_DIM)
    key_block = jnp.concatenate([span_keys, cache_keys], 0)
    value_block = jnp.concatenate([span_values, cache_values], 0)
    piece_keys = lax.all_gather(key_block, "ctx", axis=0, tiled=True)
    piece_values = lax.all_gather(value_block, "ctx", axis=0, tiled=True)
    piece_rows = piece_keys.shape[0]
    index = jnp.arange(piece_rows, dtype=jnp.int32)
    owner = index // block_rows
    within = index % block_rows
    usable = (within < token_count) | (owner * cached_rows + within - token_count < length)
    scores = (
        jnp.einsum(
            "thd,phd->htp",
            queries.reshape(token_count, head_count, HEAD_DIM),
            piece_keys.reshape(piece_rows, head_count, HEAD_DIM),
            preferred_element_type=jnp.float32,
        )
        * scaling
    )
    scores = jnp.where(usable[None, None, :], scores, -1e30)
    peak = jnp.max(scores, axis=2, keepdims=True)
    weights = jnp.where(usable[None, None, :], jnp.exp(scores - peak), 0.0)
    total = jnp.sum(weights, axis=2)
    accum = jnp.einsum(
        "htp,phd->htd",
        weights.astype(jnp.bfloat16),
        piece_values.reshape(piece_rows, head_count, HEAD_DIM),
        preferred_element_type=jnp.float32,
    )
    return (
        (accum / total[:, :, None])
        .transpose(1, 0, 2)
        .reshape(token_count, column_count)
        .astype(jnp.bfloat16)
    )


def attend_by_head(queries, span_keys, span_values, cache_keys, cache_values, length, extra):
    token_count, column_count = queries.shape
    head_count = column_count // HEAD_DIM
    cached_rows = cache_keys.shape[0]
    ctx_count = lax.axis_size("ctx")
    local_heads = head_count // ctx_count
    width = local_heads * HEAD_DIM
    scaling = 1.0 / math.sqrt(HEAD_DIM)
    block_rows = token_count + cached_rows
    sources = [queries, span_keys, cache_keys, span_values, cache_values]
    base_rows = sum(x.shape[0] for x in sources)
    packed = jnp.concatenate(
        [x.reshape(x.shape[0], ctx_count, width).transpose(1, 0, 2) for x in sources]
        + [extra],
        1,
    )
    packed_rows = packed.shape[1]
    got = lax.all_to_all(packed, "ctx", split_axis=0, concat_axis=0, tiled=True)
    got = got.reshape(ctx_count, packed_rows, local_heads, HEAD_DIM)
    query_all = got[:, :token_count].reshape(ctx_count * token_count, local_heads, HEAD_DIM)
    key_all = got[:, token_count : token_count + block_rows].reshape(
        ctx_count * block_rows, local_heads, HEAD_DIM
    )
    extra_got = got[:, base_rows:]
    value_all = got[:, token_count + block_rows : base_rows].reshape(
        ctx_count * block_rows, local_heads, HEAD_DIM
    )
    piece_rows = ctx_count * block_rows
    index = jnp.arange(piece_rows, dtype=jnp.int32)
    owner = index // block_rows
    within = index % block_rows
    usable = (within < token_count) | (owner * cached_rows + within - token_count < length)
    scores = (
        jnp.einsum("thd,phd->htp", query_all, key_all, preferred_element_type=jnp.float32)
        * scaling
    )
    scores = jnp.where(usable[None, None, :], scores, -1e30)
    peak = jnp.max(scores, axis=2, keepdims=True)
    weights = jnp.where(usable[None, None, :], jnp.exp(scores - peak), 0.0)
    total = jnp.sum(weights, axis=2)
    accum = jnp.einsum(
        "htp,phd->thd",
        weights.astype(jnp.bfloat16),
        value_all,
        preferred_element_type=jnp.float32,
    )
    head_out = (accum / total.T[:, :, None]).astype(jnp.bfloat16)
    head_out = head_out.reshape(ctx_count, token_count, width)
    back = lax.all_to_all(head_out, "ctx", split_axis=0, concat_axis=0, tiled=True)
    return back.transpose(1, 0, 2).reshape(token_count, column_count), extra_got


def on_device(
    hidden_in,
    queries,
    span_keys,
    span_values,
    cache_keys,
    cache_values,
    cache_lengths,
    slot_request,
    out_weight,
    norm_gain,
    expert_ids,
    expert_gates,
    gate_proj,
    up_proj,
    down_proj,
):
    token_count, feature_width = hidden_in.shape
    column_count = queries.shape[1]
    head_count = column_count // HEAD_DIM
    ctx_count = lax.axis_size("ctx")
    slot_place = lax.axis_index("req")
    slot_count = slot_request.shape[0]
    slot_range = jnp.arange(slot_count, dtype=jnp.int32)
    request = jnp.sum(jnp.where(slot_range == slot_place, slot_request, 0))
    length = jnp.sum(jnp.where(slot_range == request, cache_lengths, 0))
    local_experts = gate_proj.shape[0]
    expert_total = local_experts * ctx_count
    gate_matrix = jnp.sum(
        jnp.where(
            expert_ids[:, :, None] == jnp.arange(expert_total, dtype=jnp.int32)[None, None, :],
            expert_gates[:, :, None],
            0.0,
        ),
        axis=1,
    )
    first_expert = lax.axis_index("ctx") * local_experts
    if head_count % ctx_count == 0:
        width = column_count // ctx_count
        high = lax.reduce_precision(gate_matrix, exponent_bits=8, mantissa_bits=7)
        rest = gate_matrix - high
        middle = lax.reduce_precision(rest, exponent_bits=8, mantissa_bits=7)
        low = rest - middle
        parts = jnp.stack([high, middle, low], 0).astype(jnp.bfloat16)
        parts = parts.reshape(3, token_count, ctx_count, local_experts)
        parts = parts.transpose(2, 0, 3, 1).reshape(ctx_count, -1)
        part_len = parts.shape[1]
        part_rows = -(-part_len // width)
        parts = jnp.pad(parts, ((0, 0), (0, part_rows * width - part_len)))
        parts = parts.reshape(ctx_count, part_rows, width)
        attended, parts_got = attend_by_head(
            queries, span_keys, span_values, cache_keys, cache_values, length, parts
        )
        parts_got = parts_got.reshape(ctx_count, part_rows * width)[:, :part_len]
        parts_got = parts_got.reshape(ctx_count, 3, local_experts, token_count).astype(
            jnp.float32
        )
        local_gates = (
            (parts_got[:, 0] + parts_got[:, 1]) + parts_got[:, 2]
        ).transpose(1, 0, 2)
    else:
        attended = attend_gathered(
            queries, span_keys, span_values, cache_keys, cache_values, length
        )
        local_gates = lax.all_gather(
            lax.dynamic_slice_in_dim(gate_matrix, first_expert, local_experts, 1).T,
            "ctx",
            axis=1,
            tiled=True,
        ).reshape(local_experts, ctx_count, token_count)
    residual = hidden_in.astype(jnp.float32) + jnp.dot(
        attended, out_weight, preferred_element_type=jnp.float32
    )
    mean_square = jnp.mean(residual * residual, axis=1, keepdims=True)
    normed = (residual * lax.rsqrt(mean_square + 1e-06) * norm_gain).astype(jnp.bfloat16)

    def experts_on(rows, gates):
        moe = None
        for j in range(local_experts):
            gate_val = jnp.dot(rows, gate_proj[j], preferred_element_type=jnp.float32)
            up_val = jnp.dot(rows, up_proj[j], preferred_element_type=jnp.float32)
            activated = (jax.nn.silu(gate_val) * up_val).astype(jnp.bfloat16)
            activated = lax.optimization_barrier(activated)
            produced = jnp.dot(
                activated, down_proj[j], preferred_element_type=jnp.float32
            ).astype(jnp.bfloat16)
            term = gates[j][:, None] * produced.astype(jnp.float32)
            moe = term if moe is None else moe + term
        return moe

    if ctx_count & (ctx_count - 1) == 0 and ctx_count > 1 and token_count % 4 == 0:
        me = lax.axis_index("ctx")
        stream_rows = token_count // 4
        orders = xor_orders(ctx_count)
        moe_pieces = []
        earlier = None
        for group in range(2):
            firsts = [(2 * group + s) * stream_rows for s in range(2)]
            inputs = [normed[f : f + stream_rows] for f in firsts]
            if earlier is not None:
                inputs, _ = lax.optimization_barrier((inputs, earlier))
            helds = gather_xor(inputs, orders, ctx_count)
            earlier = helds
            gates = []
            for first, order in zip(firsts, orders):
                sources = jnp.array(relative_masks(order), jnp.int32) ^ me
                gates.append(
                    jnp.take(
                        local_gates[:, :, first : first + stream_rows], sources, axis=1
                    ).reshape(local_experts, ctx_count * stream_rows)
                )
            rows = jnp.concatenate(
                [held.reshape(ctx_count * stream_rows, feature_width) for held in helds], 0
            )
            part = experts_on(rows, jnp.concatenate(gates, 1))
            part = part.reshape(2, ctx_count, stream_rows, feature_width)
            moe_group = jnp.concatenate(reduce_xor([part[0], part[1]], orders, ctx_count), 0)
            final_group = (
                residual[firsts[0] : firsts[0] + 2 * stream_rows] + moe_group
            ).astype(jnp.bfloat16)
            moe_pieces.append(route_to_request(final_group, slot_request))
        return jnp.concatenate(moe_pieces, 0)
    else:
        normed_all = lax.all_gather(normed, "ctx", axis=0, tiled=True)
        moe = experts_on(normed_all, local_gates.reshape(local_experts, -1))
        moe_rows = lax.psum_scatter(
            moe.astype(jnp.bfloat16), "ctx", scatter_dimension=0, tiled=True
        ).astype(jnp.float32)
    final = (residual + moe_rows).astype(jnp.bfloat16)

    return route_to_request(final, slot_request)


def xor_orders(ctx_count):
    bits = ctx_count.bit_length() - 1
    first = list(range(bits - 1, -1, -1))
    second = list(first)
    if bits >= 3:
        second[0], second[1] = second[1], second[0]
    return [first, second]


def relative_masks(order):
    return [
        sum(((f >> step) & 1) << bit for step, bit in enumerate(order))
        for f in range(1 << len(order))
    ]


def swap(rows, mask, ctx_count):
    return lax.ppermute(rows, "ctx", [(c, c ^ mask) for c in range(ctx_count)])


def gather_xor(rows_list, orders, ctx_count):
    helds = [rows[None] for rows in rows_list]
    for step in range(len(orders[0])):
        masks = [1 << order[step] for order in orders]
        if all(mask == masks[0] for mask in masks):
            got = swap(jnp.stack(helds), masks[0], ctx_count)
            gots = [got[i] for i in range(len(helds))]
        else:
            gots = [swap(held, mask, ctx_count) for held, mask in zip(helds, masks)]
        helds = [jnp.concatenate([held, got], 0) for held, got in zip(helds, gots)]
        helds = list(lax.optimization_barrier(tuple(helds)))
    return helds


def reduce_xor(parts, orders, ctx_count):
    totals = parts
    for step in reversed(range(len(orders[0]))):
        half = totals[0].shape[0] // 2
        masks = [1 << order[step] for order in orders]
        outgoing = [total[half:].astype(jnp.bfloat16) for total in totals]
        if all(mask == masks[0] for mask in masks):
            sent = swap(jnp.stack(outgoing), masks[0], ctx_count)
            sents = [sent[i] for i in range(len(outgoing))]
        else:
            sents = [swap(out, mask, ctx_count) for out, mask in zip(outgoing, masks)]
        totals = [total[:half] + sent.astype(jnp.float32) for total, sent in zip(totals, sents)]
        totals = list(lax.optimization_barrier(tuple(totals)))
    return [total[0] for total in totals]


def route_to_request(final, slot_request):
    slot_count = slot_request.shape[0]
    token_count = final.shape[0]
    slot_range = jnp.arange(slot_count, dtype=jnp.int32)
    if slot_count <= 4:
        orders = list(itertools.permutations(range(slot_count)))
        table = jnp.array(orders, jnp.int32)
        match = jnp.all(table == slot_request[None, :], axis=1)
        choice = jnp.sum(jnp.where(match, jnp.arange(len(orders), dtype=jnp.int32), 0))

        def mover(order):
            pairs = [(g, order[g]) for g in range(slot_count)]
            if all(a == b for a, b in pairs):
                return lambda rows: rows
            return lambda rows: lax.ppermute(rows, "req", pairs)

        return lax.switch(choice, [mover(order) for order in orders], final)
    slot_place = lax.axis_index("req")
    source_slot = jnp.sum(jnp.where(slot_request == slot_place, slot_range, 0))
    piece = lax.all_gather(final, "req", axis=0, tiled=True)
    piece_rows = piece.shape[0]
    offset = source_slot * token_count
    inside = (offset >= 0) & (offset + token_count <= piece_rows)
    portion = lax.dynamic_slice_in_dim(
        piece, jnp.clip(offset, 0, piece_rows - token_count), token_count, 0
    )
    return jnp.where(inside, portion, jnp.zeros_like(final))


def solution(mesh):
    return jax.shard_map(
        on_device,
        mesh=mesh,
        in_specs=(
            P(("req", "ctx"), None),
            P(("req", "ctx"), None),
            P(("req", "ctx"), None),
            P(("req", "ctx"), None),
            P(("req", "ctx"), None),
            P(("req", "ctx"), None),
            P(),
            P(),
            P(),
            P(),
            P(("req", "ctx"), None),
            P(("req", "ctx"), None),
            P("ctx", None, None),
            P("ctx", None, None),
            P("ctx", None, None),
        ),
        out_specs=P(("req", "ctx"), None),
        check_vma=False,
    )
```

profile of v0, /device:TPU:16, one launch (start us, length us, event | category | flops | bytes accessed | tf_op | source)
XLA Modules:
  0.0 143.7 jit_solution(12884637180056883841)
XLA Ops:
  6.2 1.4 copy.91
  7.6 3.7 %all-to-all-start = ((bf16[8,774,128]{2,1,0:T(8,128)(2,1)}), bf16[8,774,128]{2,1,0:T(8,128)(2,1)S(1)}, u32[]{:S(2)}, u32[]{:S(2)}) async-start(bf16[8,774,128]{2,1,0:T(8,128)(2,1)} %copy.91), calls=%async_computation | async-start | bytes 3178496 | tf_op jit(solution)/shard_map/all_to_all | solution.py:71
  15.2 17.3 %all-to-all-done = bf16[8,774,128]{2,1,0:T(8,128)(2,1)S(1)} async-done(((bf16[8,774,128]{2,1,0:T(8,128)(2,1)}), bf16[8,774,128]{2,1,0:T(8,128)(2,1)S(1)}, u32[]{:S(2)}, u32[]{:S(2)}) %all-to-all-start) | async-done | bytes 1585184 | tf_op jit(solution)/shard_map/all_to_all | solution.py:71
  33.1 1.8 %fusion = (f32[1024]{0:T(1024)S(1)}, f32[1024,2560]{1,0:T(8,128)S(1)}) fusion(pred[2560]{0:T(1024)(128)(4,1)S(1)} %fusion.86, bf16[1024,128]{1,0:T(8,128)(2,1)S(1)} %bitcast.196, bf16[2560,128]{1,0:T(8,128)(2,1)S(1)} %bitcast.189), kind=kOutput, calls=%fused_computation.6 | convolution fusion | flops 678951936 | bytes 11409920 | tf_op jit(solution)/shard_map/thd,phd->htp/dot_general | solution.py:87
  34.9 2.7 %fusion.1 = f32[1024]{0:T(1024)S(1)} fusion(f32[1024,2560]{1,0:T(8,128)S(1)} %get-tuple-element.203, f32[1024]{0:T(1024)S(1)} %get-tuple-element.202, pred[2560]{0:T(1024)(128)(4,1)S(1)} %fusion.86), kind=kLoop, calls=%fused_computation.7 | loop fusion | flops 13106176 | bytes 10496512 | tf_op jit(solution)/shard_map/reduce_sum | solution.py:93
  37.6 3.0 %fusion.71 = bf16[16,8,8,128]{3,1,2,0:T(8,128)(2,1)S(1)} fusion(bf16[2560,128]{1,0:T(8,128)(2,1)S(1)} %bitcast.222, f32[1024,2560]{1,0:T(8,128)S(1)} %get-tuple-element.203, f32[1024]{0:T(1024)S(1)} %get-tuple-element.202, pred[2560]{0:T(1024)(128)(4,1)S(1)} %fusion.86, f32[1024]{0:T(1024)S(1)} %fusion.1), kind=kOutput, calls=%fused_computation.78 | convolution fusion | flops 684457984 | bytes 11414016 | tf_op jit(solution)/shard_map/htp,phd->thd/dot_general | solution.py:94
  41.4 3.6 %all-to-all-start.1 = ((bf16[8,128,128]{1,2,0:T(8,128)(2,1)}), bf16[8,128,128]{1,2,0:T(8,128)(2,1)S(1)}, u32[]{:S(2)}, u32[]{:S(2)}) async-start(bf16[8,128,128]{1,2,0:T(8,128)(2,1)} %copy.96), calls=%async_computation.1 | async-start | bytes 524288 | tf_op jit(solution)/shard_map/all_to_all | solution.py:102
  45.0 6.7 %all-to-all-done.1 = bf16[8,128,128]{1,2,0:T(8,128)(2,1)S(1)} async-done(((bf16[8,128,128]{1,2,0:T(8,128)(2,1)}), bf16[8,128,128]{1,2,0:T(8,128)(2,1)S(1)}, u32[]{:S(2)}, u32[]{:S(2)}) %all-to-all-start.1) | async-done | bytes 262176 | tf_op jit(solution)/shard_map/all_to_all | solution.py:102
  51.7 3.0 %multiply_reduce_fusion = (f32[128]{0:T(128)S(1)}, f32[128,2048]{1,0:T(8,128)S(1)}) fusion(bf16[128,1024]{0,1:T(8,128)(2,1)S(1)} %bitcast.199, bf16[1024,2048]{1,0:T(8,128)(2,1)} %param.79, bf16[128,2048]{1,0:T(8,128)(2,1)S(1)} %copy-done.1), kind=kOutput, calls=%fused_computation.75 | convolution fusion | flops 537919360 | bytes 6029824 | tf_op jit(solution)/shard_map/dot_general | solution.py:176
  56.2 3.8 %collective-permute-done.47 = bf16[1,32,2048]{2,1,0:T(8,128)(2,1)S(1)} collective-permute-done((bf16[1,32,2048]{2,1,0:T(8,128)(2,1)S(1)}, bf16[1,32,2048]{2,1,0:T(8,128)(2,1)S(1)}, u32[]{:S(2)}, u32[]{:S(2)}) %collective-permute-start.47) | collective-permute-done | bytes 131104 | tf_op jit(solution)/shard_map/ppermute | solution.py:256
  60.7 1.5 %collective-permute-start.48 = (bf16[2,32,2048]{2,1,0:T(8,128)(2,1)S(1)}, bf16[2,32,2048]{2,1,0:T(8,128)(2,1)S(1)}, u32[]{:S(2)}, u32[]{:S(2)}) collective-permute-start(bf16[2,32,2048]{2,1,0:T(8,128)(2,1)S(1)} %pad_maximum_fusion.15), channel_id=1, source_target_pairs={{0,2},{1,3},{2,0},{3,1},{4,6},{5,7},{6,4},{7,5},{8,10},{9,11},{10,... | collective-permute-start | bytes 786440 | tf_op jit(solution)/shard_map/ppermute | solution.py:256
  65.4 2.3 %collective-permute-done.48 = bf16[2,32,2048]{2,1,0:T(8,128)(2,1)S(1)} collective-permute-done((bf16[2,32,2048]{2,1,0:T(8,128)(2,1)S(1)}, bf16[2,32,2048]{2,1,0:T(8,128)(2,1)S(1)}, u32[]{:S(2)}, u32[]{:S(2)}) %collective-permute-start.48) | collective-permute-done | bytes 262176 | tf_op jit(solution)/shard_map/ppermute | solution.py:256
  67.8 2.1 %collective-permute-done.49 = bf16[2,32,2048]{2,1,0:T(8,128)(2,1)S(1)} collective-permute-done((bf16[2,32,2048]{2,1,0:T(8,128)(2,1)S(1)}, bf16[2,32,2048]{2,1,0:T(8,128)(2,1)S(1)}, u32[]{:S(2)}, u32[]{:S(2)}) %collective-permute-start.49) | collective-permute-done | bytes 262176 | tf_op jit(solution)/shard_map/ppermute | solution.py:256
  71.3 2.6 %collective-permute-done.50 = bf16[2,4,32,2048]{3,2,1,0:T(8,128)(2,1)S(1)} collective-permute-done((bf16[2,4,32,2048]{3,2,1,0:T(8,128)(2,1)}, bf16[2,4,32,2048]{3,2,1,0:T(8,128)(2,1)S(1)}, u32[]{:S(2)}, u32[]{:S(2)}) %collective-permute-start.50) | collective-permute-done | bytes 1048608 | tf_op jit(solution)/shard_map/ppermute | solution.py:256
  79.4 1.3 fusion.59
  82.9 1.4 fusion.103
  85.9 1.6 %collective-permute-start.59 = (bf16[2,32,2048]{2,1,0:T(8,128)(2,1)S(1)}, bf16[2,32,2048]{2,1,0:T(8,128)(2,1)S(1)}, u32[]{:S(2)}, u32[]{:S(2)}) collective-permute-start(bf16[2,32,2048]{2,1,0:T(8,128)(2,1)S(1)} %pad_maximum_fusion.18), channel_id=1, source_target_pairs={{0,4},{1,5},{2,6},{3,7},{4,0},{5,1},{6,2},{7,3},{8,12},{9,13},{10,... | collective-permute-start | bytes 786440 | tf_op jit(solution)/shard_map/ppermute | solution.py:256
  87.6 4.8 %collective-permute-done.58 = bf16[2,32,2048]{2,1,0:T(8,128)(2,1)S(1)} collective-permute-done((bf16[2,32,2048]{2,1,0:T(8,128)(2,1)S(1)}, bf16[2,32,2048]{2,1,0:T(8,128)(2,1)S(1)}, u32[]{:S(2)}, u32[]{:S(2)}) %collective-permute-start.58) | collective-permute-done | bytes 262176 | tf_op jit(solution)/shard_map/ppermute | solution.py:256
  94.3 1.6 %collective-permute-start.53 = (bf16[2,32,2048]{2,1,0:T(8,128)(2,1)S(1)}, bf16[2,32,2048]{2,1,0:T(8,128)(2,1)S(1)}, u32[]{:S(2)}, u32[]{:S(2)}) collective-permute-start(bf16[2,32,2048]{2,1,0:T(8,128)(2,1)S(1)} %slice.449), channel_id=1, source_target_pairs={{0,4},{1,5},{2,6},{3,7},{4,0},{5,1},{6,2},{7,3},{8,12},{9,13},{10,... | collective-permute-start | bytes 786440 | tf_op jit(solution)/shard_map/ppermute | solution.py:256
  99.6 1.3 fusion.50
  100.9 1.6 %fusion.56 = bf16[512,512]{1,0:T(8,128)(2,1)S(1)} fusion(bf16[2,2048,512]{2,1,0:T(8,128)(2,1)S(1)} %copy-done.9, f32[512,512]{1,0:T(8,128)S(1)} %fusion.22, bf16[256,2048]{1,0:T(8,128)(2,1)S(1)} %bitcast.205, bf16[256,2048]{1,0:T(8,128)(2,1)S(1)} %bitcast.209), kind=kOutput, calls=%fused_computation.59 | convolution fusion | flops 1079508992 | bytes 5767168 | tf_op jit(solution)/shard_map/dot_general | solution.py:186
  103.7 1.4 fusion.104
  109.6 2.0 %collective-permute-done.55 = bf16[1,32,2048]{2,1,0:T(8,128)(2,1)S(1)} collective-permute-done((bf16[1,32,2048]{2,1,0:T(8,128)(2,1)S(1)}, bf16[1,32,2048]{2,1,0:T(8,128)(2,1)S(1)}, u32[]{:S(2)}, u32[]{:S(2)}) %collective-permute-start.55) | collective-permute-done | bytes 131104 | tf_op jit(solution)/shard_map/ppermute | solution.py:256
  112.9 5.2 %collective-permute-done.63 = bf16[2,32,2048]{2,1,0:T(8,128)(2,1)S(1)} collective-permute-done((bf16[2,32,2048]{2,1,0:T(8,128)(2,1)S(1)}, bf16[2,32,2048]{2,1,0:T(8,128)(2,1)S(1)}, u32[]{:S(2)}, u32[]{:S(2)}) %collective-permute-start.63) | collective-permute-done | bytes 262176 | tf_op jit(solution)/shard_map/ppermute | solution.py:256
  118.1 1.6 %collective-permute-done.62 = bf16[2,32,2048]{2,1,0:T(8,128)(2,1)S(1)} collective-permute-done((bf16[2,32,2048]{2,1,0:T(8,128)(2,1)S(1)}, bf16[2,32,2048]{2,1,0:T(8,128)(2,1)S(1)}, u32[]{:S(2)}, u32[]{:S(2)}) %collective-permute-start.62) | collective-permute-done | bytes 262176 | tf_op jit(solution)/shard_map/ppermute | solution.py:256
  121.8 3.0 %collective-permute-done.65 = bf16[1,32,2048]{2,1,0:T(8,128)(2,1)S(1)} collective-permute-done((bf16[1,32,2048]{2,1,0:T(8,128)(2,1)S(1)}, bf16[1,32,2048]{2,1,0:T(8,128)(2,1)S(1)}, u32[]{:S(2)}, u32[]{:S(2)}) %collective-permute-start.65) | collective-permute-done | bytes 131104 | tf_op jit(solution)/shard_map/ppermute | solution.py:256
  126.2 8.4 %conditional.2 = (bf16[64,2048]{1,0:T(8,128)(2,1)S(1)}) conditional(s32[]{:T(128)} %clamp.6, bf16[64,2048]{1,0:T(8,128)(2,1)S(1)} %get-tuple-element.170, bf16[64,2048]{1,0:T(8,128)(2,1)S(1)} %get-tuple-element.170, bf16[64,2048]{1,0:T(8,128)(2,1)S(1)} %get-tuple-element.170, ...), branch_computations={%region_8.10_spmd, %region_9.11_spmd, %region_10.12_spmd, %region_... | conditional | bytes 1572912 | solution.py:305
  126.2 2.4 %collective-permute-start.1 = (bf16[64,2048]{1,0:T(8,128)(2,1)S(1)}, bf16[64,2048]{1,0:T(8,128)(2,1)S(1)}, u32[]{:S(2)}, u32[]{:S(2)}) collective-permute-start(bf16[64,2048]{1,0:T(8,128)(2,1)S(1)} %param.4), channel_id=1, source_target_pairs={{0,0},{8,16},{16,8},{24,24},{1,1},{9,17},{17,9},{25,25},{2,2},{10,... | collective-permute-start | bytes 786440 | tf_op jit(solution)/shard_map/cond/branch_2_fun/ppermute | solution.py:303
  128.6 5.9 %collective-permute-done.1 = bf16[64,2048]{1,0:T(8,128)(2,1)S(1)} collective-permute-done((bf16[64,2048]{1,0:T(8,128)(2,1)S(1)}, bf16[64,2048]{1,0:T(8,128)(2,1)S(1)}, u32[]{:S(2)}, u32[]{:S(2)}) %collective-permute-start.1) | collective-permute-done | bytes 262176 | tf_op jit(solution)/shard_map/cond/branch_2_fun/ppermute | solution.py:303
  134.5 8.4 %conditional.3 = (bf16[64,2048]{1,0:T(8,128)(2,1)S(1)}) conditional(s32[]{:T(128)} %clamp.6, bf16[64,2048]{1,0:T(8,128)(2,1)S(1)} %get-tuple-element.171, bf16[64,2048]{1,0:T(8,128)(2,1)S(1)} %get-tuple-element.171, bf16[64,2048]{1,0:T(8,128)(2,1)S(1)} %get-tuple-element.171, ...), branch_computations={%region_34.36_spmd, %region_35.37_spmd, %region_36.38_spmd, %regio... | conditional | bytes 1572912 | solution.py:305
  134.6 2.4 %collective-permute-start.24 = (bf16[64,2048]{1,0:T(8,128)(2,1)S(1)}, bf16[64,2048]{1,0:T(8,128)(2,1)S(1)}, u32[]{:S(2)}, u32[]{:S(2)}) collective-permute-start(bf16[64,2048]{1,0:T(8,128)(2,1)S(1)} %param.28), channel_id=1, source_target_pairs={{0,0},{8,16},{16,8},{24,24},{1,1},{9,17},{17,9},{25,25},{2,2},{10,... | collective-permute-start | bytes 786440 | tf_op jit(solution)/shard_map/cond/branch_2_fun/ppermute | solution.py:303
  136.9 5.9 %collective-permute-done.24 = bf16[64,2048]{1,0:T(8,128)(2,1)S(1)} collective-permute-done((bf16[64,2048]{1,0:T(8,128)(2,1)S(1)}, bf16[64,2048]{1,0:T(8,128)(2,1)S(1)}, u32[]{:S(2)}, u32[]{:S(2)}) %collective-permute-start.24) | collective-permute-done | bytes 262176 | tf_op jit(solution)/shard_map/cond/branch_2_fun/ppermute | solution.py:303
  (161 shorter events, 43.5 us)
Async XLA Ops:
  0.0 5.8 %copy-start.2 = (bf16[192,1024]{1,0:T(8,128)(2,1)S(1)}, bf16[192,1024]{1,0:T(8,128)(2,1)}, u32[]{:S(2)}) copy-start(bf16[192,1024]{1,0:T(8,128)(2,1)} %param.76) | copy-start | bytes 1179652
  6.0 5.3 %copy-start.4 = (s32[24,4]{0,1:T(4,128)S(1)}, s32[24,4]{0,1:T(4,128)}, u32[]{:S(2)}) copy-start(s32[24,4]{0,1:T(4,128)} %constant.76.clone) | copy-start | bytes 1156
  6.0 5.3 %copy-start.7 = (s32[4]{0:T(128)S(1)}, s32[4]{0:T(128)}, u32[]{:S(2)}) copy-start(s32[4]{0:T(128)} %param.78) | copy-start | bytes 52
  6.0 7.3 %copy-start.10 = (s32[4]{0:T(128)S(1)}, s32[4]{0:T(128)}, u32[]{:S(2)}) copy-start(s32[4]{0:T(128)} %param.77) | copy-start | bytes 52
  6.0 9.1 %copy-start.5 = (s32[8]{0:T(128)S(1)}, s32[8]{0:T(128)}, u32[]{:S(2)}) copy-start(s32[8]{0:T(128)} %constant.75.clone) | copy-start | bytes 100
  6.0 9.1 %copy-start.6 = (s32[8]{0:T(128)S(1)}, s32[8]{0:T(128)}, u32[]{:S(2)}) copy-start(s32[8]{0:T(128)} %constant.74.clone) | copy-start | bytes 100
  7.6 24.9 %all-to-all-start = ((bf16[8,774,128]{2,1,0:T(8,128)(2,1)}), bf16[8,774,128]{2,1,0:T(8,128)(2,1)S(1)}, u32[]{:S(2)}, u32[]{:S(2)}) async-start(bf16[8,774,128]{2,1,0:T(8,128)(2,1)} %copy.91), calls=%async_computation | async-start | bytes 3178496 | tf_op jit(solution)/shard_map/all_to_all | solution.py:71
  37.6 14.1 %copy-start.1 = (bf16[128,2048]{1,0:T(8,128)(2,1)S(1)}, bf16[128,2048]{1,0:T(8,128)(2,1)}, u32[]{:S(2)}) copy-start(bf16[128,2048]{1,0:T(8,128)(2,1)} %param.71) | copy-start | bytes 1572868
  40.6 14.1 %copy-start.3 = (f32[2048]{0:T(1024)S(1)}, f32[2048]{0:T(1024)}, u32[]{:S(2)}) copy-start(f32[2048]{0:T(1024)} %param.80) | copy-start | bytes 24580
  41.4 10.3 %all-to-all-start.1 = ((bf16[8,128,128]{1,2,0:T(8,128)(2,1)}), bf16[8,128,128]{1,2,0:T(8,128)(2,1)S(1)}, u32[]{:S(2)}, u32[]{:S(2)}) async-start(bf16[8,128,128]{1,2,0:T(8,128)(2,1)} %copy.96), calls=%async_computation.1 | async-start | bytes 524288 | tf_op jit(solution)/shard_map/all_to_all | solution.py:102
  54.9 5.0 %collective-permute-start.47 = (bf16[1,32,2048]{2,1,0:T(8,128)(2,1)S(1)}, bf16[1,32,2048]{2,1,0:T(8,128)(2,1)S(1)}, u32[]{:S(2)}, u32[]{:S(2)}) collective-permute-start(bf16[1,32,2048]{2,1,0:T(8,128)(2,1)S(1)} %get-tuple-element.180), channel_id=1, source_target_pairs={{0,2},{1,3},{2,0},{3,1},{4,6},{5,7},{6,4},{7,5},{8,10},{9,11},{10,... | collective-permute-start | bytes 393224 | tf_op jit(solution)/shard_map/ppermute | solution.py:256
  55.6 5.1 %collective-permute-start.46 = (bf16[1,32,2048]{2,1,0:T(8,128)(2,1)S(1)}, bf16[1,32,2048]{2,1,0:T(8,128)(2,1)S(1)}, u32[]{:S(2)}, u32[]{:S(2)}) collective-permute-start(bf16[1,32,2048]{2,1,0:T(8,128)(2,1)S(1)} %get-tuple-element.183), channel_id=1, source_target_pairs={{0,4},{1,5},{2,6},{3,7},{4,0},{5,1},{6,2},{7,3},{8,12},{9,13},{10,... | collective-permute-start | bytes 393224 | tf_op jit(solution)/shard_map/ppermute | solution.py:256
  60.7 7.0 %collective-permute-start.48 = (bf16[2,32,2048]{2,1,0:T(8,128)(2,1)S(1)}, bf16[2,32,2048]{2,1,0:T(8,128)(2,1)S(1)}, u32[]{:S(2)}, u32[]{:S(2)}) collective-permute-start(bf16[2,32,2048]{2,1,0:T(8,128)(2,1)S(1)} %pad_maximum_fusion.15), channel_id=1, source_target_pairs={{0,2},{1,3},{2,0},{3,1},{4,6},{5,7},{6,4},{7,5},{8,10},{9,11},{10,... | collective-permute-start | bytes 786440 | tf_op jit(solution)/shard_map/ppermute | solution.py:256
  63.4 6.4 %collective-permute-start.49 = (bf16[2,32,2048]{2,1,0:T(8,128)(2,1)S(1)}, bf16[2,32,2048]{2,1,0:T(8,128)(2,1)S(1)}, u32[]{:S(2)}, u32[]{:S(2)}) collective-permute-start(bf16[2,32,2048]{2,1,0:T(8,128)(2,1)S(1)} %pad_maximum_fusion.16), channel_id=1, source_target_pairs={{0,4},{1,5},{2,6},{3,7},{4,0},{5,1},{6,2},{7,3},{8,12},{9,13},{10,... | collective-permute-start | bytes 786440 | tf_op jit(solution)/shard_map/ppermute | solution.py:256
  71.0 2.9 %collective-permute-start.50 = (bf16[2,4,32,2048]{3,2,1,0:T(8,128)(2,1)}, bf16[2,4,32,2048]{3,2,1,0:T(8,128)(2,1)S(1)}, u32[]{:S(2)}, u32[]{:S(2)}) collective-permute-start(bf16[2,4,32,2048]{3,2,1,0:T(8,128)(2,1)} %pad_maximum_fusion.2), channel_id=1, source_target_pairs={{0,1},{1,0},{2,3},{3,2},{4,5},{5,4},{6,7},{7,6},{8,9},{9,8},{10,11... | collective-permute-start | bytes 3145736 | tf_op jit(solution)/shard_map/ppermute | solution.py:256
  76.7 7.6 %collective-permute-start.57 = (bf16[1,32,2048]{2,1,0:T(8,128)(2,1)S(1)}, bf16[1,32,2048]{2,1,0:T(8,128)(2,1)S(1)}, u32[]{:S(2)}, u32[]{:S(2)}) collective-permute-start(bf16[1,32,2048]{2,1,0:T(8,128)(2,1)S(1)} %bitcast.225), channel_id=1, source_target_pairs={{0,2},{1,3},{2,0},{3,1},{4,6},{5,7},{6,4},{7,5},{8,10},{9,11},{10,... | collective-permute-start | bytes 393224 | tf_op jit(solution)/shard_map/ppermute | solution.py:256
  77.7 6.7 %collective-permute-start.56 = (bf16[1,32,2048]{2,1,0:T(8,128)(2,1)S(1)}, bf16[1,32,2048]{2,1,0:T(8,128)(2,1)S(1)}, u32[]{:S(2)}, u32[]{:S(2)}) collective-permute-start(bf16[1,32,2048]{2,1,0:T(8,128)(2,1)S(1)} %bitcast.223), channel_id=1, source_target_pairs={{0,4},{1,5},{2,6},{3,7},{4,0},{5,1},{6,2},{7,3},{8,12},{9,13},{10,... | collective-permute-start | bytes 393224 | tf_op jit(solution)/shard_map/ppermute | solution.py:256
  84.4 8.0 %collective-permute-start.58 = (bf16[2,32,2048]{2,1,0:T(8,128)(2,1)S(1)}, bf16[2,32,2048]{2,1,0:T(8,128)(2,1)S(1)}, u32[]{:S(2)}, u32[]{:S(2)}) collective-permute-start(bf16[2,32,2048]{2,1,0:T(8,128)(2,1)S(1)} %pad_maximum_fusion.17), channel_id=1, source_target_pairs={{0,2},{1,3},{2,0},{3,1},{4,6},{5,7},{6,4},{7,5},{8,10},{9,11},{10,... | collective-permute-start | bytes 786440 | tf_op jit(solution)/shard_map/ppermute | solution.py:256
  85.9 7.6 %collective-permute-start.59 = (bf16[2,32,2048]{2,1,0:T(8,128)(2,1)S(1)}, bf16[2,32,2048]{2,1,0:T(8,128)(2,1)S(1)}, u32[]{:S(2)}, u32[]{:S(2)}) collective-permute-start(bf16[2,32,2048]{2,1,0:T(8,128)(2,1)S(1)} %pad_maximum_fusion.18), channel_id=1, source_target_pairs={{0,4},{1,5},{2,6},{3,7},{4,0},{5,1},{6,2},{7,3},{8,12},{9,13},{10,... | collective-permute-start | bytes 786440 | tf_op jit(solution)/shard_map/ppermute | solution.py:256
  87.5 6.4 %collective-permute-start.51 = (bf16[2,4,32,2048]{3,2,1,0:T(8,128)(2,1)S(1)}, bf16[2,4,32,2048]{3,2,1,0:T(8,128)(2,1)S(1)}, u32[]{:S(2)}, u32[]{:S(2)}) collective-permute-start(bf16[2,4,32,2048]{3,2,1,0:T(8,128)(2,1)S(1)} %pad_maximum_fusion.5), channel_id=1, source_target_pairs={{0,1},{1,0},{2,3},{3,2},{4,5},{5,4},{6,7},{7,6},{8,9},{9,8},{10,11... | collective-permute-start | bytes 3145736 | tf_op jit(solution)/shard_map/ppermute | solution.py:256
  93.6 3.2 %collective-permute-start.60 = (bf16[2,4,32,2048]{3,2,1,0:T(8,128)(2,1)S(1)}, bf16[2,4,32,2048]{3,2,1,0:T(8,128)(2,1)S(1)}, u32[]{:S(2)}, u32[]{:S(2)}) collective-permute-start(bf16[2,4,32,2048]{3,2,1,0:T(8,128)(2,1)S(1)} %pad_maximum_fusion.6), channel_id=1, source_target_pairs={{0,1},{1,0},{2,3},{3,2},{4,5},{5,4},{6,7},{7,6},{8,9},{9,8},{10,11... | collective-permute-start | bytes 3145736 | tf_op jit(solution)/shard_map/ppermute | solution.py:256
  94.3 11.2 %collective-permute-start.53 = (bf16[2,32,2048]{2,1,0:T(8,128)(2,1)S(1)}, bf16[2,32,2048]{2,1,0:T(8,128)(2,1)S(1)}, u32[]{:S(2)}, u32[]{:S(2)}) collective-permute-start(bf16[2,32,2048]{2,1,0:T(8,128)(2,1)S(1)} %slice.449), channel_id=1, source_target_pairs={{0,4},{1,5},{2,6},{3,7},{4,0},{5,1},{6,2},{7,3},{8,12},{9,13},{10,... | collective-permute-start | bytes 786440 | tf_op jit(solution)/shard_map/ppermute | solution.py:256
  95.8 9.7 %collective-permute-start.52 = (bf16[2,32,2048]{2,1,0:T(8,128)(2,1)S(1)}, bf16[2,32,2048]{2,1,0:T(8,128)(2,1)S(1)}, u32[]{:S(2)}, u32[]{:S(2)}) collective-permute-start(bf16[2,32,2048]{2,1,0:T(8,128)(2,1)S(1)} %slice.450), channel_id=1, source_target_pairs={{0,2},{1,3},{2,0},{3,1},{4,6},{5,7},{6,4},{7,5},{8,10},{9,11},{10,... | collective-permute-start | bytes 786440 | tf_op jit(solution)/shard_map/ppermute | solution.py:256
  105.4 2.7 %collective-permute-start.61 = (bf16[2,4,32,2048]{3,2,1,0:T(8,128)(2,1)S(1)}, bf16[2,4,32,2048]{3,2,1,0:T(8,128)(2,1)S(1)}, u32[]{:S(2)}, u32[]{:S(2)}) collective-permute-start(bf16[2,4,32,2048]{3,2,1,0:T(8,128)(2,1)S(1)} %pad_maximum_fusion.9), channel_id=1, source_target_pairs={{0,1},{1,0},{2,3},{3,2},{4,5},{5,4},{6,7},{7,6},{8,9},{9,8},{10,11... | collective-permute-start | bytes 3145736 | tf_op jit(solution)/shard_map/ppermute | solution.py:256
  105.7 6.0 %collective-permute-start.55 = (bf16[1,32,2048]{2,1,0:T(8,128)(2,1)S(1)}, bf16[1,32,2048]{2,1,0:T(8,128)(2,1)S(1)}, u32[]{:S(2)}, u32[]{:S(2)}) collective-permute-start(bf16[1,32,2048]{2,1,0:T(8,128)(2,1)S(1)} %slice.453), channel_id=1, source_target_pairs={{0,2},{1,3},{2,0},{3,1},{4,6},{5,7},{6,4},{7,5},{8,10},{9,11},{10,... | collective-permute-start | bytes 393224 | tf_op jit(solution)/shard_map/ppermute | solution.py:256
  106.8 14.1 %collective-permute-start.54 = (bf16[1,32,2048]{2,1,0:T(8,128)(2,1)S(1)}, bf16[1,32,2048]{2,1,0:T(8,128)(2,1)S(1)}, u32[]{:S(2)}, u32[]{:S(2)}) collective-permute-start(bf16[1,32,2048]{2,1,0:T(8,128)(2,1)S(1)} %slice.454), channel_id=1, source_target_pairs={{0,4},{1,5},{2,6},{3,7},{4,0},{5,1},{6,2},{7,3},{8,12},{9,13},{10,... | collective-permute-start | bytes 393224 | tf_op jit(solution)/shard_map/ppermute | solution.py:256
  108.5 9.5 %collective-permute-start.63 = (bf16[2,32,2048]{2,1,0:T(8,128)(2,1)S(1)}, bf16[2,32,2048]{2,1,0:T(8,128)(2,1)S(1)}, u32[]{:S(2)}, u32[]{:S(2)}) collective-permute-start(bf16[2,32,2048]{2,1,0:T(8,128)(2,1)S(1)} %slice.447), channel_id=1, source_target_pairs={{0,4},{1,5},{2,6},{3,7},{4,0},{5,1},{6,2},{7,3},{8,12},{9,13},{10,... | collective-permute-start | bytes 786440 | tf_op jit(solution)/shard_map/ppermute | solution.py:256
  111.7 8.0 %collective-permute-start.62 = (bf16[2,32,2048]{2,1,0:T(8,128)(2,1)S(1)}, bf16[2,32,2048]{2,1,0:T(8,128)(2,1)S(1)}, u32[]{:S(2)}, u32[]{:S(2)}) collective-permute-start(bf16[2,32,2048]{2,1,0:T(8,128)(2,1)S(1)} %slice.448), channel_id=1, source_target_pairs={{0,2},{1,3},{2,0},{3,1},{4,6},{5,7},{6,4},{7,5},{8,10},{9,11},{10,... | collective-permute-start | bytes 786440 | tf_op jit(solution)/shard_map/ppermute | solution.py:256
  119.7 5.0 %collective-permute-start.65 = (bf16[1,32,2048]{2,1,0:T(8,128)(2,1)S(1)}, bf16[1,32,2048]{2,1,0:T(8,128)(2,1)S(1)}, u32[]{:S(2)}, u32[]{:S(2)}) collective-permute-start(bf16[1,32,2048]{2,1,0:T(8,128)(2,1)S(1)} %slice.451), channel_id=1, source_target_pairs={{0,2},{1,3},{2,0},{3,1},{4,6},{5,7},{6,4},{7,5},{8,10},{9,11},{10,... | collective-permute-start | bytes 393224 | tf_op jit(solution)/shard_map/ppermute | solution.py:256
  121.0 5.0 %collective-permute-start.64 = (bf16[1,32,2048]{2,1,0:T(8,128)(2,1)S(1)}, bf16[1,32,2048]{2,1,0:T(8,128)(2,1)S(1)}, u32[]{:S(2)}, u32[]{:S(2)}) collective-permute-start(bf16[1,32,2048]{2,1,0:T(8,128)(2,1)S(1)} %slice.452), channel_id=1, source_target_pairs={{0,4},{1,5},{2,6},{3,7},{4,0},{5,1},{6,2},{7,3},{8,12},{9,13},{10,... | collective-permute-start | bytes 393224 | tf_op jit(solution)/shard_map/ppermute | solution.py:256
  126.2 8.3 %collective-permute-start.1 = (bf16[64,2048]{1,0:T(8,128)(2,1)S(1)}, bf16[64,2048]{1,0:T(8,128)(2,1)S(1)}, u32[]{:S(2)}, u32[]{:S(2)}) collective-permute-start(bf16[64,2048]{1,0:T(8,128)(2,1)S(1)} %param.4), channel_id=1, source_target_pairs={{0,0},{8,16},{16,8},{24,24},{1,1},{9,17},{17,9},{25,25},{2,2},{10,... | collective-permute-start | bytes 786440 | tf_op jit(solution)/shard_map/cond/branch_2_fun/ppermute | solution.py:303
  134.6 8.3 %collective-permute-start.24 = (bf16[64,2048]{1,0:T(8,128)(2,1)S(1)}, bf16[64,2048]{1,0:T(8,128)(2,1)S(1)}, u32[]{:S(2)}, u32[]{:S(2)}) collective-permute-start(bf16[64,2048]{1,0:T(8,128)(2,1)S(1)} %param.28), channel_id=1, source_target_pairs={{0,0},{8,16},{16,8},{24,24},{1,1},{9,17},{17,9},{25,25},{2,2},{10,... | collective-permute-start | bytes 786440 | tf_op jit(solution)/shard_map/cond/branch_2_fun/ppermute | solution.py:303
  (3 other events, 7.7 us)
where the time goes:
time: 145 us; the launch traced here: 144 us
  waiting for transfers between devices  66 us (46%)
  starting transfers between devices  28.7 us (20%)
  matrix products  23.9 us (16%)
  local copies, waits for them, and re-layouts  12.6 us (9%)
  other arithmetic  10.9 us (8%)
  between operations  1.49 us (1%)
    ppermute x20, waiting for transfers between devices, swap(): return lax.ppermute(rows, 'ctx', [(c, c ^ mask) for c in range(ctx_count)])  30.2 us
    all_to_all x1, waiting for transfers between devices, attend_by_head(): got = lax.all_to_all(packed, 'ctx', split_axis=0, concat_axis=0, tiled=True)  17.3 us
    ppermute x20, starting transfers between devices, swap(): return lax.ppermute(rows, 'ctx', [(c, c ^ mask) for c in range(ctx_count)])  16.7 us
    ppermute x2, waiting for transfers between devices, mover(): return lambda rows: lax.ppermute(rows, 'req', pairs)  11.8 us
    all_to_all x1, waiting for transfers between devices, attend_by_head(): lax.all_to_all(head_out, 'ctx', split_axis=0, concat_axis=0, tiled=True)  6.66 us
    unnamed x35, local copies, waits for them, and re-layouts  5.61 us
    dot_general x4, matrix products, experts_on(): up_val = jnp.dot(rows, up_proj[j], preferred_element_type=jnp.float32)  5.6 us
    dot_general x4, matrix products, experts_on(): jnp.dot(activated, down_proj[j], preferred_element_type=jnp.float32)  5.41 us
  transfers between devices with their start and end apart: 24, of which 17 were waited for; matrix products, arithmetic and copies ran while one was open for 15% of the time, Pallas kernels for 0%

commit v1 on v0

--- a/solution.py
+++ b/solution.py
@@ -219,12 +219,8 @@
             )
             part = experts_on(rows, jnp.concatenate(gates, 1))
             part = part.reshape(2, ctx_count, stream_rows, feature_width)
-            moe_group = jnp.concatenate(reduce_xor([part[0], part[1]], orders, ctx_count), 0)
-            final_group = (
-                residual[firsts[0] : firsts[0] + 2 * stream_rows] + moe_group
-            ).astype(jnp.bfloat16)
-            moe_pieces.append(route_to_request(final_group, slot_request))
-        return jnp.concatenate(moe_pieces, 0)
+            moe_pieces.extend(reduce_xor([part[0], part[1]], orders, ctx_count))
+        moe_rows = jnp.concatenate(moe_pieces, 0)
     else:
         normed_all = lax.all_gather(normed, "ctx", axis=0, tiled=True)
         moe = experts_on(normed_all, local_gates.reshape(local_experts, -1))

time: 145 us -> 143 us (0.986)
  the two profiles are of different devices: /device:TPU:16 before, /device:TPU:24 now
where the time goes in v1:
time: 143 us; the launch traced here: 141 us
  waiting for transfers between devices  66 us (46%)
  starting transfers between devices  26.4 us (18%)
  matrix products  23.9 us (17%)
  local copies, waits for them, and re-layouts  13.4 us (9%)
  other arithmetic  10.2 us (7%)
  between operations  1.49 us (1%)
    ppermute x20, waiting for transfers between devices, swap(): return lax.ppermute(rows, 'ctx', [(c, c ^ mask) for c in range(ctx_count)])  30.2 us
    all_to_all x1, waiting for transfers between devices, attend_by_head(): got = lax.all_to_all(packed, 'ctx', split_axis=0, concat_axis=0, tiled=True)  17.2 us
    ppermute x20, starting transfers between devices, swap(): return lax.ppermute(rows, 'ctx', [(c, c ^ mask) for c in range(ctx_count)])  16.7 us
    ppermute x1, waiting for transfers between devices, mover(): return lambda rows: lax.ppermute(rows, 'req', pairs)  11.9 us
    all_to_all x1, waiting for transfers between devices, attend_by_head(): lax.all_to_all(head_out, 'ctx', split_axis=0, concat_axis=0, tiled=True)  6.66 us
    unnamed x37, local copies, waits for them, and re-layouts  6.4 us
    dot_general x4, matrix products, experts_on(): up_val = jnp.dot(rows, up_proj[j], preferred_element_type=jnp.float32)  5.6 us
    dot_general x4, matrix products, experts_on(): jnp.dot(activated, down_proj[j], preferred_element_type=jnp.float32)  5.42 us
  transfers between devices with their start and end apart: 23, of which 16 were waited for; matrix products, arithmetic and copies ran while one was open for 16% of the time, Pallas kernels for 0%

profile of v1, /device:TPU:24, one launch (start us, length us, event | category | flops | bytes accessed | tf_op | source)
XLA Modules:
  0.0 141.5 jit_solution(10114300305571156056)
XLA Ops:
  6.2 1.4 copy.114
  7.6 3.7 %all-to-all-start = ((bf16[8,774,128]{2,1,0:T(8,128)(2,1)}), bf16[8,774,128]{2,1,0:T(8,128)(2,1)S(1)}, u32[]{:S(2)}, u32[]{:S(2)}) async-start(bf16[8,774,128]{2,1,0:T(8,128)(2,1)} %copy.114), calls=%async_computation | async-start | bytes 3178496 | tf_op jit(solution)/shard_map/all_to_all | solution.py:71
  15.3 17.2 %all-to-all-done = bf16[8,774,128]{2,1,0:T(8,128)(2,1)S(1)} async-done(((bf16[8,774,128]{2,1,0:T(8,128)(2,1)}), bf16[8,774,128]{2,1,0:T(8,128)(2,1)S(1)}, u32[]{:S(2)}, u32[]{:S(2)}) %all-to-all-start) | async-done | bytes 1585184 | tf_op jit(solution)/shard_map/all_to_all | solution.py:71
  33.1 1.8 %fusion = (f32[1024]{0:T(1024)S(1)}, f32[1024,2560]{1,0:T(8,128)S(1)}) fusion(pred[2560]{0:T(1024)(128)(4,1)S(1)} %fusion.85, bf16[1024,128]{1,0:T(8,128)(2,1)S(1)} %bitcast.196, bf16[2560,128]{1,0:T(8,128)(2,1)S(1)} %bitcast.189), kind=kOutput, calls=%fused_computation.6 | convolution fusion | flops 678951936 | bytes 11409920 | tf_op jit(solution)/shard_map/thd,phd->htp/dot_general | solution.py:87
  35.0 2.7 %fusion.1 = f32[1024]{0:T(1024)S(1)} fusion(f32[1024,2560]{1,0:T(8,128)S(1)} %get-tuple-element.153, f32[1024]{0:T(1024)S(1)} %get-tuple-element.152, pred[2560]{0:T(1024)(128)(4,1)S(1)} %fusion.85), kind=kLoop, calls=%fused_computation.7 | loop fusion | flops 13106176 | bytes 10496512 | tf_op jit(solution)/shard_map/reduce_sum | solution.py:93
  37.7 3.0 %fusion.72 = bf16[16,8,8,128]{3,1,2,0:T(8,128)(2,1)S(1)} fusion(bf16[2560,128]{1,0:T(8,128)(2,1)S(1)} %bitcast.222, f32[1024,2560]{1,0:T(8,128)S(1)} %get-tuple-element.153, f32[1024]{0:T(1024)S(1)} %get-tuple-element.152, pred[2560]{0:T(1024)(128)(4,1)S(1)} %fusion.85, f32[1024]{0:T(1024)S(1)} %fusion.1), kind=kOutput, calls=%fused_computation.80 | convolution fusion | flops 684457984 | bytes 11414016 | tf_op jit(solution)/shard_map/htp,phd->thd/dot_general | solution.py:94
  41.5 3.6 %all-to-all-start.1 = ((bf16[8,128,128]{1,2,0:T(8,128)(2,1)}), bf16[8,128,128]{1,2,0:T(8,128)(2,1)S(1)}, u32[]{:S(2)}, u32[]{:S(2)}) async-start(bf16[8,128,128]{1,2,0:T(8,128)(2,1)} %copy.119), calls=%async_computation.1 | async-start | bytes 524288 | tf_op jit(solution)/shard_map/all_to_all | solution.py:102
  45.1 6.7 %all-to-all-done.1 = bf16[8,128,128]{1,2,0:T(8,128)(2,1)S(1)} async-done(((bf16[8,128,128]{1,2,0:T(8,128)(2,1)}), bf16[8,128,128]{1,2,0:T(8,128)(2,1)S(1)}, u32[]{:S(2)}, u32[]{:S(2)}) %all-to-all-start.1) | async-done | bytes 262176 | tf_op jit(solution)/shard_map/all_to_all | solution.py:102
  51.8 3.0 %multiply_reduce_fusion = (f32[128]{0:T(128)S(1)}, f32[128,2048]{1,0:T(8,128)S(1)}) fusion(bf16[128,1024]{0,1:T(8,128)(2,1)S(1)} %bitcast.199, bf16[1024,2048]{1,0:T(8,128)(2,1)} %param.54, bf16[128,2048]{1,0:T(8,128)(2,1)S(1)} %copy-done.1), kind=kOutput, calls=%fused_computation.77 | convolution fusion | flops 537919360 | bytes 6029824 | tf_op jit(solution)/shard_map/dot_general | solution.py:176
  56.3 3.8 %collective-permute-done.24 = bf16[1,32,2048]{2,1,0:T(8,128)(2,1)S(1)} collective-permute-done((bf16[1,32,2048]{2,1,0:T(8,128)(2,1)S(1)}, bf16[1,32,2048]{2,1,0:T(8,128)(2,1)S(1)}, u32[]{:S(2)}, u32[]{:S(2)}) %collective-permute-start.24) | collective-permute-done | bytes 131104 | tf_op jit(solution)/shard_map/ppermute | solution.py:252
  60.8 1.5 %collective-permute-start.25 = (bf16[2,32,2048]{2,1,0:T(8,128)(2,1)S(1)}, bf16[2,32,2048]{2,1,0:T(8,128)(2,1)S(1)}, u32[]{:S(2)}, u32[]{:S(2)}) collective-permute-start(bf16[2,32,2048]{2,1,0:T(8,128)(2,1)S(1)} %pad_maximum_fusion.14), channel_id=1, source_target_pairs={{0,2},{1,3},{2,0},{3,1},{4,6},{5,7},{6,4},{7,5},{8,10},{9,11},{10,... | collective-permute-start | bytes 786440 | tf_op jit(solution)/shard_map/ppermute | solution.py:252
  65.5 2.3 %collective-permute-done.25 = bf16[2,32,2048]{2,1,0:T(8,128)(2,1)S(1)} collective-permute-done((bf16[2,32,2048]{2,1,0:T(8,128)(2,1)S(1)}, bf16[2,32,2048]{2,1,0:T(8,128)(2,1)S(1)}, u32[]{:S(2)}, u32[]{:S(2)}) %collective-permute-start.25) | collective-permute-done | bytes 262176 | tf_op jit(solution)/shard_map/ppermute | solution.py:252
  67.8 2.1 %collective-permute-done.26 = bf16[2,32,2048]{2,1,0:T(8,128)(2,1)S(1)} collective-permute-done((bf16[2,32,2048]{2,1,0:T(8,128)(2,1)S(1)}, bf16[2,32,2048]{2,1,0:T(8,128)(2,1)S(1)}, u32[]{:S(2)}, u32[]{:S(2)}) %collective-permute-start.26) | collective-permute-done | bytes 262176 | tf_op jit(solution)/shard_map/ppermute | solution.py:252
  71.4 2.6 %collective-permute-done.27 = bf16[2,4,32,2048]{3,2,1,0:T(8,128)(2,1)S(1)} collective-permute-done((bf16[2,4,32,2048]{3,2,1,0:T(8,128)(2,1)}, bf16[2,4,32,2048]{3,2,1,0:T(8,128)(2,1)S(1)}, u32[]{:S(2)}, u32[]{:S(2)}) %collective-permute-start.27) | collective-permute-done | bytes 1048608 | tf_op jit(solution)/shard_map/ppermute | solution.py:252
  78.1 1.3 fusion.53
  79.5 1.4 fusion.59
  81.7 1.3 convolution_convert_fusion.3
  83.0 1.4 %fusion.103 = (bf16[512,2048]{1,0:T(8,128)(2,1)S(1)}, f32[512,2048]{1,0:T(8,128)S(1)}) fusion(bf16[512,512]{1,0:T(8,128)(2,1)S(1)} %fusion.53, bf16[2,512,2048]{2,1,0:T(8,128)(2,1)S(1)} %copy-done, f32[512]{0:T(512)S(1)} %bitcast.232, bf16[512,2048]{1,0:T(8,128)(2,1)S(1)} %convolution_convert_fusion.3, f32[512]{0:T(512)S(1)} %bitcast.231), kind=kOutput, calls=%fused_computation.183 | convolution fusion | flops 1081081856 | bytes 11014144 | tf_op jit(solution)/shard_map/dot_general | solution.py:189
  84.5 1.3 collective-permute-start.35
  85.9 1.6 %collective-permute-start.36 = (bf16[2,32,2048]{2,1,0:T(8,128)(2,1)S(1)}, bf16[2,32,2048]{2,1,0:T(8,128)(2,1)S(1)}, u32[]{:S(2)}, u32[]{:S(2)}) collective-permute-start(bf16[2,32,2048]{2,1,0:T(8,128)(2,1)S(1)} %pad_maximum_fusion.17), channel_id=1, source_target_pairs={{0,4},{1,5},{2,6},{3,7},{4,0},{5,1},{6,2},{7,3},{8,12},{9,13},{10,... | collective-permute-start | bytes 786440 | tf_op jit(solution)/shard_map/ppermute | solution.py:252
  87.7 4.8 %collective-permute-done.35 = bf16[2,32,2048]{2,1,0:T(8,128)(2,1)S(1)} collective-permute-done((bf16[2,32,2048]{2,1,0:T(8,128)(2,1)S(1)}, bf16[2,32,2048]{2,1,0:T(8,128)(2,1)S(1)}, u32[]{:S(2)}, u32[]{:S(2)}) %collective-permute-start.35) | collective-permute-done | bytes 262176 | tf_op jit(solution)/shard_map/ppermute | solution.py:252
  94.4 1.6 %collective-permute-start.30 = (bf16[2,32,2048]{2,1,0:T(8,128)(2,1)S(1)}, bf16[2,32,2048]{2,1,0:T(8,128)(2,1)S(1)}, u32[]{:S(2)}, u32[]{:S(2)}) collective-permute-start(bf16[2,32,2048]{2,1,0:T(8,128)(2,1)S(1)} %slice.433), channel_id=1, source_target_pairs={{0,4},{1,5},{2,6},{3,7},{4,0},{5,1},{6,2},{7,3},{8,12},{9,13},{10,... | collective-permute-start | bytes 786440 | tf_op jit(solution)/shard_map/ppermute | solution.py:252
  99.6 1.3 fusion.50
  101.0 1.6 %fusion.56 = bf16[512,512]{1,0:T(8,128)(2,1)S(1)} fusion(bf16[2,2048,512]{2,1,0:T(8,128)(2,1)S(1)} %copy-done.10, f32[512,512]{1,0:T(8,128)S(1)} %fusion.22, bf16[256,2048]{1,0:T(8,128)(2,1)S(1)} %bitcast.205, bf16[256,2048]{1,0:T(8,128)(2,1)S(1)} %bitcast.209), kind=kOutput, calls=%fused_computation.59 | convolution fusion | flops 1079508992 | bytes 5767168 | tf_op jit(solution)/shard_map/dot_general | solution.py:186
  103.8 1.4 %fusion.102 = (bf16[512,2048]{1,0:T(8,128)(2,1)S(1)}, f32[512,2048]{1,0:T(8,128)S(1)}) fusion(bf16[512,512]{1,0:T(8,128)(2,1)S(1)} %fusion.50, bf16[2,512,2048]{2,1,0:T(8,128)(2,1)S(1)} %copy-done, f32[512]{0:T(512)S(1)} %bitcast.230, bf16[512,2048]{1,0:T(8,128)(2,1)S(1)} %convolution_convert_fusion.1, f32[512]{0:T(512)S(1)} %bitcast.229), kind=kOutput, calls=%fused_computation.182 | convolution fusion | flops 1081081856 | bytes 11014144 | tf_op jit(solution)/shard_map/dot_general | solution.py:189
  109.7 2.0 %collective-permute-done.32 = bf16[1,32,2048]{2,1,0:T(8,128)(2,1)S(1)} collective-permute-done((bf16[1,32,2048]{2,1,0:T(8,128)(2,1)S(1)}, bf16[1,32,2048]{2,1,0:T(8,128)(2,1)S(1)}, u32[]{:S(2)}, u32[]{:S(2)}) %collective-permute-start.32) | collective-permute-done | bytes 131104 | tf_op jit(solution)/shard_map/ppermute | solution.py:252
  112.9 5.2 %collective-permute-done.40 = bf16[2,32,2048]{2,1,0:T(8,128)(2,1)S(1)} collective-permute-done((bf16[2,32,2048]{2,1,0:T(8,128)(2,1)S(1)}, bf16[2,32,2048]{2,1,0:T(8,128)(2,1)S(1)}, u32[]{:S(2)}, u32[]{:S(2)}) %collective-permute-start.40) | collective-permute-done | bytes 262176 | tf_op jit(solution)/shard_map/ppermute | solution.py:252
  118.2 1.6 %collective-permute-done.39 = bf16[2,32,2048]{2,1,0:T(8,128)(2,1)S(1)} collective-permute-done((bf16[2,32,2048]{2,1,0:T(8,128)(2,1)S(1)}, bf16[2,32,2048]{2,1,0:T(8,128)(2,1)S(1)}, u32[]{:S(2)}, u32[]{:S(2)}) %collective-permute-start.39) | collective-permute-done | bytes 262176 | tf_op jit(solution)/shard_map/ppermute | solution.py:252
  121.8 3.0 %collective-permute-done.42 = bf16[1,32,2048]{2,1,0:T(8,128)(2,1)S(1)} collective-permute-done((bf16[1,32,2048]{2,1,0:T(8,128)(2,1)S(1)}, bf16[1,32,2048]{2,1,0:T(8,128)(2,1)S(1)}, u32[]{:S(2)}, u32[]{:S(2)}) %collective-permute-start.42) | collective-permute-done | bytes 131104 | tf_op jit(solution)/shard_map/ppermute | solution.py:252
  126.3 14.4 %conditional.1 = (bf16[128,2048]{1,0:T(8,128)(2,1)S(1)}) conditional(s32[]{:T(128)} %clamp.3, bf16[128,2048]{1,0:T(8,128)(2,1)S(1)} %fusion.65, bf16[128,2048]{1,0:T(8,128)(2,1)S(1)} %fusion.65, bf16[128,2048]{1,0:T(8,128)(2,1)S(1)} %fusion.65, bf16[128,2048]{1,0:T(8,128)(2,1)S(1)} %fusion.65, ...), branch_computations={%region_8.10_spmd, %region_9.11_spmd, %region_10.12_spmd, %region_... | conditional | bytes 3145776 | solution.py:301
  126.3 2.4 %collective-permute-start.3 = (bf16[128,2048]{1,0:T(8,128)(2,1)S(1)}, bf16[128,2048]{1,0:T(8,128)(2,1)S(1)}, u32[]{:S(2)}, u32[]{:S(2)}) collective-permute-start(bf16[128,2048]{1,0:T(8,128)(2,1)S(1)} %param.6), channel_id=1, source_target_pairs={{0,0},{8,24},{16,8},{24,16},{1,1},{9,25},{17,9},{25,17},{2,2},{10,... | collective-permute-start | bytes 1572872 | tf_op jit(solution)/shard_map/cond/branch_4_fun/ppermute | solution.py:299
  128.7 11.9 %collective-permute-done.3 = bf16[128,2048]{1,0:T(8,128)(2,1)S(1)} collective-permute-done((bf16[128,2048]{1,0:T(8,128)(2,1)S(1)}, bf16[128,2048]{1,0:T(8,128)(2,1)S(1)}, u32[]{:S(2)}, u32[]{:S(2)}) %collective-permute-start.3) | collective-permute-done | bytes 524320 | tf_op jit(solution)/shard_map/cond/branch_4_fun/ppermute | solution.py:299
  (158 shorter events, 39.6 us)
Async XLA Ops:
  0.0 5.8 %copy-start.3 = (bf16[192,1024]{1,0:T(8,128)(2,1)S(1)}, bf16[192,1024]{1,0:T(8,128)(2,1)}, u32[]{:S(2)}) copy-start(bf16[192,1024]{1,0:T(8,128)(2,1)} %param.51) | copy-start | bytes 1179652
  6.0 5.4 %copy-start.5 = (s32[24,4]{0,1:T(4,128)S(1)}, s32[24,4]{0,1:T(4,128)}, u32[]{:S(2)}) copy-start(s32[24,4]{0,1:T(4,128)} %constant.76.clone) | copy-start | bytes 1156
  6.0 5.4 %copy-start.8 = (s32[4]{0:T(128)S(1)}, s32[4]{0:T(128)}, u32[]{:S(2)}) copy-start(s32[4]{0:T(128)} %param.53) | copy-start | bytes 52
  6.0 7.4 %copy-start.11 = (s32[4]{0:T(128)S(1)}, s32[4]{0:T(128)}, u32[]{:S(2)}) copy-start(s32[4]{0:T(128)} %param.52) | copy-start | bytes 52
  6.0 9.2 %copy-start.6 = (s32[8]{0:T(128)S(1)}, s32[8]{0:T(128)}, u32[]{:S(2)}) copy-start(s32[8]{0:T(128)} %constant.75.clone) | copy-start | bytes 100
  6.0 9.2 %copy-start.7 = (s32[8]{0:T(128)S(1)}, s32[8]{0:T(128)}, u32[]{:S(2)}) copy-start(s32[8]{0:T(128)} %constant.74.clone) | copy-start | bytes 100
  7.6 24.9 %all-to-all-start = ((bf16[8,774,128]{2,1,0:T(8,128)(2,1)}), bf16[8,774,128]{2,1,0:T(8,128)(2,1)S(1)}, u32[]{:S(2)}, u32[]{:S(2)}) async-start(bf16[8,774,128]{2,1,0:T(8,128)(2,1)} %copy.114), calls=%async_computation | async-start | bytes 3178496 | tf_op jit(solution)/shard_map/all_to_all | solution.py:71
  37.6 14.1 %copy-start.1 = (bf16[128,2048]{1,0:T(8,128)(2,1)S(1)}, bf16[128,2048]{1,0:T(8,128)(2,1)}, u32[]{:S(2)}) copy-start(bf16[128,2048]{1,0:T(8,128)(2,1)} %param.46) | copy-start | bytes 1572868
  40.7 14.1 %copy-start.4 = (f32[2048]{0:T(1024)S(1)}, f32[2048]{0:T(1024)}, u32[]{:S(2)}) copy-start(f32[2048]{0:T(1024)} %param.55) | copy-start | bytes 24580
  41.5 10.3 %all-to-all-start.1 = ((bf16[8,128,128]{1,2,0:T(8,128)(2,1)}), bf16[8,128,128]{1,2,0:T(8,128)(2,1)S(1)}, u32[]{:S(2)}, u32[]{:S(2)}) async-start(bf16[8,128,128]{1,2,0:T(8,128)(2,1)} %copy.119), calls=%async_computation.1 | async-start | bytes 524288 | tf_op jit(solution)/shard_map/all_to_all | solution.py:102
  55.0 5.0 %collective-permute-start.24 = (bf16[1,32,2048]{2,1,0:T(8,128)(2,1)S(1)}, bf16[1,32,2048]{2,1,0:T(8,128)(2,1)S(1)}, u32[]{:S(2)}, u32[]{:S(2)}) collective-permute-start(bf16[1,32,2048]{2,1,0:T(8,128)(2,1)S(1)} %get-tuple-element.130), channel_id=1, source_target_pairs={{0,2},{1,3},{2,0},{3,1},{4,6},{5,7},{6,4},{7,5},{8,10},{9,11},{10,... | collective-permute-start | bytes 393224 | tf_op jit(solution)/shard_map/ppermute | solution.py:252
  55.6 5.1 %collective-permute-start.23 = (bf16[1,32,2048]{2,1,0:T(8,128)(2,1)S(1)}, bf16[1,32,2048]{2,1,0:T(8,128)(2,1)S(1)}, u32[]{:S(2)}, u32[]{:S(2)}) collective-permute-start(bf16[1,32,2048]{2,1,0:T(8,128)(2,1)S(1)} %get-tuple-element.133), channel_id=1, source_target_pairs={{0,4},{1,5},{2,6},{3,7},{4,0},{5,1},{6,2},{7,3},{8,12},{9,13},{10,... | collective-permute-start | bytes 393224 | tf_op jit(solution)/shard_map/ppermute | solution.py:252
  60.8 7.0 %collective-permute-start.25 = (bf16[2,32,2048]{2,1,0:T(8,128)(2,1)S(1)}, bf16[2,32,2048]{2,1,0:T(8,128)(2,1)S(1)}, u32[]{:S(2)}, u32[]{:S(2)}) collective-permute-start(bf16[2,32,2048]{2,1,0:T(8,128)(2,1)S(1)} %pad_maximum_fusion.14), channel_id=1, source_target_pairs={{0,2},{1,3},{2,0},{3,1},{4,6},{5,7},{6,4},{7,5},{8,10},{9,11},{10,... | collective-permute-start | bytes 786440 | tf_op jit(solution)/shard_map/ppermute | solution.py:252
  63.5 6.4 %collective-permute-start.26 = (bf16[2,32,2048]{2,1,0:T(8,128)(2,1)S(1)}, bf16[2,32,2048]{2,1,0:T(8,128)(2,1)S(1)}, u32[]{:S(2)}, u32[]{:S(2)}) collective-permute-start(bf16[2,32,2048]{2,1,0:T(8,128)(2,1)S(1)} %pad_maximum_fusion.15), channel_id=1, source_target_pairs={{0,4},{1,5},{2,6},{3,7},{4,0},{5,1},{6,2},{7,3},{8,12},{9,13},{10,... | collective-permute-start | bytes 786440 | tf_op jit(solution)/shard_map/ppermute | solution.py:252
  71.1 2.9 %collective-permute-start.27 = (bf16[2,4,32,2048]{3,2,1,0:T(8,128)(2,1)}, bf16[2,4,32,2048]{3,2,1,0:T(8,128)(2,1)S(1)}, u32[]{:S(2)}, u32[]{:S(2)}) collective-permute-start(bf16[2,4,32,2048]{3,2,1,0:T(8,128)(2,1)} %pad_maximum_fusion.2), channel_id=1, source_target_pairs={{0,1},{1,0},{2,3},{3,2},{4,5},{5,4},{6,7},{7,6},{8,9},{9,8},{10,11... | collective-permute-start | bytes 3145736 | tf_op jit(solution)/shard_map/ppermute | solution.py:252
  71.3 2.9 %copy-start.9 = (bf16[2,2048,512]{2,1,0:T(8,128)(2,1)S(1)}, bf16[2,2048,512]{2,1,0:T(8,128)(2,1)}, u32[]{:S(2)}) copy-start(bf16[2,2048,512]{2,1,0:T(8,128)(2,1)} %param.58) | copy-start | bytes 12582916
  76.8 7.6 %collective-permute-start.34 = (bf16[1,32,2048]{2,1,0:T(8,128)(2,1)S(1)}, bf16[1,32,2048]{2,1,0:T(8,128)(2,1)S(1)}, u32[]{:S(2)}, u32[]{:S(2)}) collective-permute-start(bf16[1,32,2048]{2,1,0:T(8,128)(2,1)S(1)} %bitcast.225), channel_id=1, source_target_pairs={{0,2},{1,3},{2,0},{3,1},{4,6},{5,7},{6,4},{7,5},{8,10},{9,11},{10,... | collective-permute-start | bytes 393224 | tf_op jit(solution)/shard_map/ppermute | solution.py:252
  77.8 6.7 %collective-permute-start.33 = (bf16[1,32,2048]{2,1,0:T(8,128)(2,1)S(1)}, bf16[1,32,2048]{2,1,0:T(8,128)(2,1)S(1)}, u32[]{:S(2)}, u32[]{:S(2)}) collective-permute-start(bf16[1,32,2048]{2,1,0:T(8,128)(2,1)S(1)} %bitcast.223), channel_id=1, source_target_pairs={{0,4},{1,5},{2,6},{3,7},{4,0},{5,1},{6,2},{7,3},{8,12},{9,13},{10,... | collective-permute-start | bytes 393224 | tf_op jit(solution)/shard_map/ppermute | solution.py:252
  84.5 8.0 %collective-permute-start.35 = (bf16[2,32,2048]{2,1,0:T(8,128)(2,1)S(1)}, bf16[2,32,2048]{2,1,0:T(8,128)(2,1)S(1)}, u32[]{:S(2)}, u32[]{:S(2)}) collective-permute-start(bf16[2,32,2048]{2,1,0:T(8,128)(2,1)S(1)} %pad_maximum_fusion.16), channel_id=1, source_target_pairs={{0,2},{1,3},{2,0},{3,1},{4,6},{5,7},{6,4},{7,5},{8,10},{9,11},{10,... | collective-permute-start | bytes 786440 | tf_op jit(solution)/shard_map/ppermute | solution.py:252
  85.9 7.6 %collective-permute-start.36 = (bf16[2,32,2048]{2,1,0:T(8,128)(2,1)S(1)}, bf16[2,32,2048]{2,1,0:T(8,128)(2,1)S(1)}, u32[]{:S(2)}, u32[]{:S(2)}) collective-permute-start(bf16[2,32,2048]{2,1,0:T(8,128)(2,1)S(1)} %pad_maximum_fusion.17), channel_id=1, source_target_pairs={{0,4},{1,5},{2,6},{3,7},{4,0},{5,1},{6,2},{7,3},{8,12},{9,13},{10,... | collective-permute-start | bytes 786440 | tf_op jit(solution)/shard_map/ppermute | solution.py:252
  87.6 6.4 %collective-permute-start.28 = (bf16[2,4,32,2048]{3,2,1,0:T(8,128)(2,1)S(1)}, bf16[2,4,32,2048]{3,2,1,0:T(8,128)(2,1)S(1)}, u32[]{:S(2)}, u32[]{:S(2)}) collective-permute-start(bf16[2,4,32,2048]{3,2,1,0:T(8,128)(2,1)S(1)} %pad_maximum_fusion.5), channel_id=1, source_target_pairs={{0,1},{1,0},{2,3},{3,2},{4,5},{5,4},{6,7},{7,6},{8,9},{9,8},{10,11... | collective-permute-start | bytes 3145736 | tf_op jit(solution)/shard_map/ppermute | solution.py:252
  93.7 3.2 %collective-permute-start.37 = (bf16[2,4,32,2048]{3,2,1,0:T(8,128)(2,1)S(1)}, bf16[2,4,32,2048]{3,2,1,0:T(8,128)(2,1)S(1)}, u32[]{:S(2)}, u32[]{:S(2)}) collective-permute-start(bf16[2,4,32,2048]{3,2,1,0:T(8,128)(2,1)S(1)} %pad_maximum_fusion.6), channel_id=1, source_target_pairs={{0,1},{1,0},{2,3},{3,2},{4,5},{5,4},{6,7},{7,6},{8,9},{9,8},{10,11... | collective-permute-start | bytes 3145736 | tf_op jit(solution)/shard_map/ppermute | solution.py:252
  94.4 11.2 %collective-permute-start.30 = (bf16[2,32,2048]{2,1,0:T(8,128)(2,1)S(1)}, bf16[2,32,2048]{2,1,0:T(8,128)(2,1)S(1)}, u32[]{:S(2)}, u32[]{:S(2)}) collective-permute-start(bf16[2,32,2048]{2,1,0:T(8,128)(2,1)S(1)} %slice.433), channel_id=1, source_target_pairs={{0,4},{1,5},{2,6},{3,7},{4,0},{5,1},{6,2},{7,3},{8,12},{9,13},{10,... | collective-permute-start | bytes 786440 | tf_op jit(solution)/shard_map/ppermute | solution.py:252
  95.9 9.7 %collective-permute-start.29 = (bf16[2,32,2048]{2,1,0:T(8,128)(2,1)S(1)}, bf16[2,32,2048]{2,1,0:T(8,128)(2,1)S(1)}, u32[]{:S(2)}, u32[]{:S(2)}) collective-permute-start(bf16[2,32,2048]{2,1,0:T(8,128)(2,1)S(1)} %slice.434), channel_id=1, source_target_pairs={{0,2},{1,3},{2,0},{3,1},{4,6},{5,7},{6,4},{7,5},{8,10},{9,11},{10,... | collective-permute-start | bytes 786440 | tf_op jit(solution)/shard_map/ppermute | solution.py:252
  105.5 2.7 %collective-permute-start.38 = (bf16[2,4,32,2048]{3,2,1,0:T(8,128)(2,1)S(1)}, bf16[2,4,32,2048]{3,2,1,0:T(8,128)(2,1)S(1)}, u32[]{:S(2)}, u32[]{:S(2)}) collective-permute-start(bf16[2,4,32,2048]{3,2,1,0:T(8,128)(2,1)S(1)} %pad_maximum_fusion.9), channel_id=1, source_target_pairs={{0,1},{1,0},{2,3},{3,2},{4,5},{5,4},{6,7},{7,6},{8,9},{9,8},{10,11... | collective-permute-start | bytes 3145736 | tf_op jit(solution)/shard_map/ppermute | solution.py:252
  105.7 6.0 %collective-permute-start.32 = (bf16[1,32,2048]{2,1,0:T(8,128)(2,1)S(1)}, bf16[1,32,2048]{2,1,0:T(8,128)(2,1)S(1)}, u32[]{:S(2)}, u32[]{:S(2)}) collective-permute-start(bf16[1,32,2048]{2,1,0:T(8,128)(2,1)S(1)} %slice.437), channel_id=1, source_target_pairs={{0,2},{1,3},{2,0},{3,1},{4,6},{5,7},{6,4},{7,5},{8,10},{9,11},{10,... | collective-permute-start | bytes 393224 | tf_op jit(solution)/shard_map/ppermute | solution.py:252
  106.9 14.1 %collective-permute-start.31 = (bf16[1,32,2048]{2,1,0:T(8,128)(2,1)S(1)}, bf16[1,32,2048]{2,1,0:T(8,128)(2,1)S(1)}, u32[]{:S(2)}, u32[]{:S(2)}) collective-permute-start(bf16[1,32,2048]{2,1,0:T(8,128)(2,1)S(1)} %slice.438), channel_id=1, source_target_pairs={{0,4},{1,5},{2,6},{3,7},{4,0},{5,1},{6,2},{7,3},{8,12},{9,13},{10,... | collective-permute-start | bytes 393224 | tf_op jit(solution)/shard_map/ppermute | solution.py:252
  108.6 9.5 %collective-permute-start.40 = (bf16[2,32,2048]{2,1,0:T(8,128)(2,1)S(1)}, bf16[2,32,2048]{2,1,0:T(8,128)(2,1)S(1)}, u32[]{:S(2)}, u32[]{:S(2)}) collective-permute-start(bf16[2,32,2048]{2,1,0:T(8,128)(2,1)S(1)} %slice.431), channel_id=1, source_target_pairs={{0,4},{1,5},{2,6},{3,7},{4,0},{5,1},{6,2},{7,3},{8,12},{9,13},{10,... | collective-permute-start | bytes 786440 | tf_op jit(solution)/shard_map/ppermute | solution.py:252
  111.8 8.0 %collective-permute-start.39 = (bf16[2,32,2048]{2,1,0:T(8,128)(2,1)S(1)}, bf16[2,32,2048]{2,1,0:T(8,128)(2,1)S(1)}, u32[]{:S(2)}, u32[]{:S(2)}) collective-permute-start(bf16[2,32,2048]{2,1,0:T(8,128)(2,1)S(1)} %slice.432), channel_id=1, source_target_pairs={{0,2},{1,3},{2,0},{3,1},{4,6},{5,7},{6,4},{7,5},{8,10},{9,11},{10,... | collective-permute-start | bytes 786440 | tf_op jit(solution)/shard_map/ppermute | solution.py:252
  119.8 5.0 %collective-permute-start.42 = (bf16[1,32,2048]{2,1,0:T(8,128)(2,1)S(1)}, bf16[1,32,2048]{2,1,0:T(8,128)(2,1)S(1)}, u32[]{:S(2)}, u32[]{:S(2)}) collective-permute-start(bf16[1,32,2048]{2,1,0:T(8,128)(2,1)S(1)} %slice.435), channel_id=1, source_target_pairs={{0,2},{1,3},{2,0},{3,1},{4,6},{5,7},{6,4},{7,5},{8,10},{9,11},{10,... | collective-permute-start | bytes 393224 | tf_op jit(solution)/shard_map/ppermute | solution.py:252
  121.0 5.0 %collective-permute-start.41 = (bf16[1,32,2048]{2,1,0:T(8,128)(2,1)S(1)}, bf16[1,32,2048]{2,1,0:T(8,128)(2,1)S(1)}, u32[]{:S(2)}, u32[]{:S(2)}) collective-permute-start(bf16[1,32,2048]{2,1,0:T(8,128)(2,1)S(1)} %slice.436), channel_id=1, source_target_pairs={{0,4},{1,5},{2,6},{3,7},{4,0},{5,1},{6,2},{7,3},{8,12},{9,13},{10,... | collective-permute-start | bytes 393224 | tf_op jit(solution)/shard_map/ppermute | solution.py:252
  126.3 14.3 %collective-permute-start.3 = (bf16[128,2048]{1,0:T(8,128)(2,1)S(1)}, bf16[128,2048]{1,0:T(8,128)(2,1)S(1)}, u32[]{:S(2)}, u32[]{:S(2)}) collective-permute-start(bf16[128,2048]{1,0:T(8,128)(2,1)S(1)} %param.6), channel_id=1, source_target_pairs={{0,0},{8,24},{16,8},{24,16},{1,1},{9,25},{17,9},{25,17},{2,2},{10,... | collective-permute-start | bytes 1572872 | tf_op jit(solution)/shard_map/cond/branch_4_fun/ppermute | solution.py:299
  (3 other events, 5.6 us)

commit v2 on v1

--- a/solution.py
+++ b/solution.py
@@ -199,6 +199,8 @@
         orders = xor_orders(ctx_count)
         moe_pieces = []
         earlier = None
+        pending = None
+        steps = len(orders[0])
         for group in range(2):
             firsts = [(2 * group + s) * stream_rows for s in range(2)]
             inputs = [normed[f : f + stream_rows] for f in firsts]
@@ -217,9 +219,13 @@
             rows = jnp.concatenate(
                 [held.reshape(ctx_count * stream_rows, feature_width) for held in helds], 0
             )
+            if pending is not None:
+                rows, pending = lax.optimization_barrier((rows, pending))
+                moe_pieces.extend(reduce_xor(pending, orders, ctx_count, steps - 1))
             part = experts_on(rows, jnp.concatenate(gates, 1))
             part = part.reshape(2, ctx_count, stream_rows, feature_width)
-            moe_pieces.extend(reduce_xor([part[0], part[1]], orders, ctx_count))
+            pending = reduce_xor([part[0], part[1]], orders, ctx_count, steps, steps - 1)
+        moe_pieces.extend(reduce_xor(pending, orders, ctx_count, steps - 1))
         moe_rows = jnp.concatenate(moe_pieces, 0)
     else:
         normed_all = lax.all_gather(normed, "ctx", axis=0, tiled=True)
@@ -266,9 +272,10 @@
     return helds
 
 
-def reduce_xor(parts, orders, ctx_count):
+def reduce_xor(parts, orders, ctx_count, start=None, stop=0):
     totals = parts
-    for step in reversed(range(len(orders[0]))):
+    start = len(orders[0]) if start is None else start
+    for step in reversed(range(stop, start)):
         half = totals[0].shape[0] // 2
         masks = [1 << order[step] for order in orders]
         outgoing = [total[half:].astype(jnp.bfloat16) for total in totals]
@@ -279,6 +286,8 @@
             sents = [swap(out, mask, ctx_count) for out, mask in zip(outgoing, masks)]
         totals = [total[:half] + sent.astype(jnp.float32) for total, sent in zip(totals, sents)]
         totals = list(lax.optimization_barrier(tuple(totals)))
+    if stop > 0:
+        return totals
     return [total[0] for total in totals]
 
 

time: 143 us -> 144 us (level)
  the two profiles are of different devices: /device:TPU:24 before, /device:TPU:16 now
where the time goes in v2:
time: 144 us; the launch traced here: 141 us
  waiting for transfers between devices  64.3 us (45%)
  starting transfers between devices  27.6 us (19%)
  matrix products  23.8 us (17%)
  local copies, waits for them, and re-layouts  13.4 us (9%)
  other arithmetic  10.4 us (7%)
  between operations  1.49 us (1%)
    ppermute x20, waiting for transfers between devices, swap(): return lax.ppermute(rows, 'ctx', [(c, c ^ mask) for c in range(ctx_count)])  31.6 us
    all_to_all x1, waiting for transfers between devices, attend_by_head(): got = lax.all_to_all(packed, 'ctx', split_axis=0, concat_axis=0, tiled=True)  17.2 us
    ppermute x20, starting transfers between devices, swap(): return lax.ppermute(rows, 'ctx', [(c, c ^ mask) for c in range(ctx_count)])  16.8 us
    ppermute x1, waiting for transfers between devices, mover(): return lambda rows: lax.ppermute(rows, 'req', pairs)  8.84 us
    all_to_all x1, waiting for transfers between devices, attend_by_head(): lax.all_to_all(head_out, 'ctx', split_axis=0, concat_axis=0, tiled=True)  6.66 us
    unnamed x37, local copies, waits for them, and re-layouts  6.4 us
    dot_general x4, matrix products, experts_on(): up_val = jnp.dot(rows, up_proj[j], preferred_element_type=jnp.float32)  5.57 us
    dot_general x4, matrix products, experts_on(): jnp.dot(activated, down_proj[j], preferred_element_type=jnp.float32)  5.41 us
  transfers between devices with their start and end apart: 23, of which 17 were waited for; matrix products, arithmetic and copies ran while one was open for 14% of the time, Pallas kernels for 0%

profile of v2, /device:TPU:16, one launch (start us, length us, event | category | flops | bytes accessed | tf_op | source)
XLA Modules:
  0.0 141.2 jit_solution(6738342267287397991)
XLA Ops:
  6.2 1.4 copy.114
  7.6 3.7 %all-to-all-start = ((bf16[8,774,128]{2,1,0:T(8,128)(2,1)}), bf16[8,774,128]{2,1,0:T(8,128)(2,1)S(1)}, u32[]{:S(2)}, u32[]{:S(2)}) async-start(bf16[8,774,128]{2,1,0:T(8,128)(2,1)} %copy.114), calls=%async_computation | async-start | bytes 3178496 | tf_op jit(solution)/shard_map/all_to_all | solution.py:71
  15.3 17.2 %all-to-all-done = bf16[8,774,128]{2,1,0:T(8,128)(2,1)S(1)} async-done(((bf16[8,774,128]{2,1,0:T(8,128)(2,1)}), bf16[8,774,128]{2,1,0:T(8,128)(2,1)S(1)}, u32[]{:S(2)}, u32[]{:S(2)}) %all-to-all-start) | async-done | bytes 1585184 | tf_op jit(solution)/shard_map/all_to_all | solution.py:71
  33.1 1.8 %fusion = (f32[1024]{0:T(1024)S(1)}, f32[1024,2560]{1,0:T(8,128)S(1)}) fusion(pred[2560]{0:T(1024)(128)(4,1)S(1)} %fusion.85, bf16[1024,128]{1,0:T(8,128)(2,1)S(1)} %bitcast.202, bf16[2560,128]{1,0:T(8,128)(2,1)S(1)} %bitcast.195), kind=kOutput, calls=%fused_computation.6 | convolution fusion | flops 678951936 | bytes 11409920 | tf_op jit(solution)/shard_map/thd,phd->htp/dot_general | solution.py:87
  35.0 2.7 %fusion.1 = f32[1024]{0:T(1024)S(1)} fusion(f32[1024,2560]{1,0:T(8,128)S(1)} %get-tuple-element.159, f32[1024]{0:T(1024)S(1)} %get-tuple-element.158, pred[2560]{0:T(1024)(128)(4,1)S(1)} %fusion.85), kind=kLoop, calls=%fused_computation.7 | loop fusion | flops 13106176 | bytes 10496512 | tf_op jit(solution)/shard_map/reduce_sum | solution.py:93
  37.6 3.0 %fusion.72 = bf16[16,8,8,128]{3,1,2,0:T(8,128)(2,1)S(1)} fusion(bf16[2560,128]{1,0:T(8,128)(2,1)S(1)} %bitcast.220, f32[1024,2560]{1,0:T(8,128)S(1)} %get-tuple-element.159, f32[1024]{0:T(1024)S(1)} %get-tuple-element.158, pred[2560]{0:T(1024)(128)(4,1)S(1)} %fusion.85, f32[1024]{0:T(1024)S(1)} %fusion.1), kind=kOutput, calls=%fused_computation.80 | convolution fusion | flops 684457984 | bytes 11414016 | tf_op jit(solution)/shard_map/htp,phd->thd/dot_general | solution.py:94
  41.5 3.6 %all-to-all-start.1 = ((bf16[8,128,128]{1,2,0:T(8,128)(2,1)}), bf16[8,128,128]{1,2,0:T(8,128)(2,1)S(1)}, u32[]{:S(2)}, u32[]{:S(2)}) async-start(bf16[8,128,128]{1,2,0:T(8,128)(2,1)} %copy.119), calls=%async_computation.1 | async-start | bytes 524288 | tf_op jit(solution)/shard_map/all_to_all | solution.py:102
  45.1 6.7 %all-to-all-done.1 = bf16[8,128,128]{1,2,0:T(8,128)(2,1)S(1)} async-done(((bf16[8,128,128]{1,2,0:T(8,128)(2,1)}), bf16[8,128,128]{1,2,0:T(8,128)(2,1)S(1)}, u32[]{:S(2)}, u32[]{:S(2)}) %all-to-all-start.1) | async-done | bytes 262176 | tf_op jit(solution)/shard_map/all_to_all | solution.py:102
  51.8 3.0 %multiply_reduce_fusion = (f32[128]{0:T(128)S(1)}, f32[128,2048]{1,0:T(8,128)S(1)}) fusion(bf16[128,1024]{0,1:T(8,128)(2,1)S(1)} %bitcast.205, bf16[1024,2048]{1,0:T(8,128)(2,1)} %param.54, bf16[128,2048]{1,0:T(8,128)(2,1)S(1)} %copy-done.1), kind=kOutput, calls=%fused_computation.77 | convolution fusion | flops 537919360 | bytes 6029824 | tf_op jit(solution)/shard_map/dot_general | solution.py:176
  56.2 3.8 %collective-permute-done.24 = bf16[1,32,2048]{2,1,0:T(8,128)(2,1)S(1)} collective-permute-done((bf16[1,32,2048]{2,1,0:T(8,128)(2,1)S(1)}, bf16[1,32,2048]{2,1,0:T(8,128)(2,1)S(1)}, u32[]{:S(2)}, u32[]{:S(2)}) %collective-permute-start.24) | collective-permute-done | bytes 131104 | tf_op jit(solution)/shard_map/ppermute | solution.py:258
  60.8 1.5 %collective-permute-start.25 = (bf16[2,32,2048]{2,1,0:T(8,128)(2,1)S(1)}, bf16[2,32,2048]{2,1,0:T(8,128)(2,1)S(1)}, u32[]{:S(2)}, u32[]{:S(2)}) collective-permute-start(bf16[2,32,2048]{2,1,0:T(8,128)(2,1)S(1)} %pad_maximum_fusion.14), channel_id=1, source_target_pairs={{0,2},{1,3},{2,0},{3,1},{4,6},{5,7},{6,4},{7,5},{8,10},{9,11},{10,... | collective-permute-start | bytes 786440 | tf_op jit(solution)/shard_map/ppermute | solution.py:258
  65.5 2.3 %collective-permute-done.25 = bf16[2,32,2048]{2,1,0:T(8,128)(2,1)S(1)} collective-permute-done((bf16[2,32,2048]{2,1,0:T(8,128)(2,1)S(1)}, bf16[2,32,2048]{2,1,0:T(8,128)(2,1)S(1)}, u32[]{:S(2)}, u32[]{:S(2)}) %collective-permute-start.25) | collective-permute-done | bytes 262176 | tf_op jit(solution)/shard_map/ppermute | solution.py:258
  67.8 2.1 %collective-permute-done.26 = bf16[2,32,2048]{2,1,0:T(8,128)(2,1)S(1)} collective-permute-done((bf16[2,32,2048]{2,1,0:T(8,128)(2,1)S(1)}, bf16[2,32,2048]{2,1,0:T(8,128)(2,1)S(1)}, u32[]{:S(2)}, u32[]{:S(2)}) %collective-permute-start.26) | collective-permute-done | bytes 262176 | tf_op jit(solution)/shard_map/ppermute | solution.py:258
  71.4 2.6 %collective-permute-done.27 = bf16[2,4,32,2048]{3,2,1,0:T(8,128)(2,1)S(1)} collective-permute-done((bf16[2,4,32,2048]{3,2,1,0:T(8,128)(2,1)}, bf16[2,4,32,2048]{3,2,1,0:T(8,128)(2,1)S(1)}, u32[]{:S(2)}, u32[]{:S(2)}) %collective-permute-start.27) | collective-permute-done | bytes 1048608 | tf_op jit(solution)/shard_map/ppermute | solution.py:258
  78.1 1.3 fusion.53
  79.5 1.4 fusion.59
  83.0 1.4 %fusion.102 = (bf16[512,2048]{1,0:T(8,128)(2,1)S(1)}, f32[512,2048]{1,0:T(8,128)S(1)}) fusion(bf16[512,512]{1,0:T(8,128)(2,1)S(1)} %fusion.53, bf16[2,512,2048]{2,1,0:T(8,128)(2,1)S(1)} %copy-done, f32[512]{0:T(512)S(1)} %bitcast.230, bf16[512,2048]{1,0:T(8,128)(2,1)S(1)} %convolution_convert_fusion.3, f32[512]{0:T(512)S(1)} %bitcast.229), kind=kOutput, calls=%fused_computation.182 | convolution fusion | flops 1081081856 | bytes 11014144 | tf_op jit(solution)/shard_map/dot_general | solution.py:189
  85.9 1.6 %collective-permute-start.31 = (bf16[2,32,2048]{2,1,0:T(8,128)(2,1)S(1)}, bf16[2,32,2048]{2,1,0:T(8,128)(2,1)S(1)}, u32[]{:S(2)}, u32[]{:S(2)}) collective-permute-start(bf16[2,32,2048]{2,1,0:T(8,128)(2,1)S(1)} %pad_maximum_fusion.17), channel_id=1, source_target_pairs={{0,4},{1,5},{2,6},{3,7},{4,0},{5,1},{6,2},{7,3},{8,12},{9,13},{10,... | collective-permute-start | bytes 786440 | tf_op jit(solution)/shard_map/ppermute | solution.py:258
  87.7 4.8 %collective-permute-done.30 = bf16[2,32,2048]{2,1,0:T(8,128)(2,1)S(1)} collective-permute-done((bf16[2,32,2048]{2,1,0:T(8,128)(2,1)S(1)}, bf16[2,32,2048]{2,1,0:T(8,128)(2,1)S(1)}, u32[]{:S(2)}, u32[]{:S(2)}) %collective-permute-start.30) | collective-permute-done | bytes 262176 | tf_op jit(solution)/shard_map/ppermute | solution.py:258
  94.3 2.1 %collective-permute-done.32 = bf16[2,4,32,2048]{3,2,1,0:T(8,128)(2,1)S(1)} collective-permute-done((bf16[2,4,32,2048]{3,2,1,0:T(8,128)(2,1)S(1)}, bf16[2,4,32,2048]{3,2,1,0:T(8,128)(2,1)S(1)}, u32[]{:S(2)}, u32[]{:S(2)}) %collective-permute-start.32) | collective-permute-done | bytes 1048608 | tf_op jit(solution)/shard_map/ppermute | solution.py:258
  99.5 1.6 %collective-permute-start.35 = (bf16[2,32,2048]{2,1,0:T(8,128)(2,1)S(1)}, bf16[2,32,2048]{2,1,0:T(8,128)(2,1)S(1)}, u32[]{:S(2)}, u32[]{:S(2)}) collective-permute-start(bf16[2,32,2048]{2,1,0:T(8,128)(2,1)S(1)} %slice.433), channel_id=1, source_target_pairs={{0,4},{1,5},{2,6},{3,7},{4,0},{5,1},{6,2},{7,3},{8,12},{9,13},{10,... | collective-permute-start | bytes 786440 | tf_op jit(solution)/shard_map/ppermute | solution.py:258
  103.3 1.5 %fusion.56 = bf16[512,512]{1,0:T(8,128)(2,1)S(1)} fusion(bf16[512,2048]{1,0:T(8,128)(2,1)S(1)} %pad_maximum_fusion, bf16[2,2048,512]{2,1,0:T(8,128)(2,1)S(1)} %copy-done.10, f32[512,512]{1,0:T(8,128)S(1)} %fusion.22), kind=kOutput, calls=%fused_computation.59 | convolution fusion | flops 1075314688 | bytes 5767168 | tf_op jit(solution)/shard_map/dot_general | solution.py:186
  106.1 1.4 %fusion.103 = (bf16[512,2048]{1,0:T(8,128)(2,1)S(1)}, f32[512,2048]{1,0:T(8,128)S(1)}) fusion(bf16[512,512]{1,0:T(8,128)(2,1)S(1)} %fusion.50, bf16[2,512,2048]{2,1,0:T(8,128)(2,1)S(1)} %copy-done, f32[512]{0:T(512)S(1)} %bitcast.228, bf16[512,2048]{1,0:T(8,128)(2,1)S(1)} %convolution_convert_fusion.1, f32[512]{0:T(512)S(1)} %bitcast.227), kind=kOutput, calls=%fused_computation.183 | convolution fusion | flops 1081081856 | bytes 11014144 | tf_op jit(solution)/shard_map/dot_general | solution.py:189
  111.1 1.6 %collective-permute-start.40 = (bf16[2,32,2048]{2,1,0:T(8,128)(2,1)S(1)}, bf16[2,32,2048]{2,1,0:T(8,128)(2,1)S(1)}, u32[]{:S(2)}, u32[]{:S(2)}) collective-permute-start(bf16[2,32,2048]{2,1,0:T(8,128)(2,1)S(1)} %slice.431), channel_id=1, source_target_pairs={{0,4},{1,5},{2,6},{3,7},{4,0},{5,1},{6,2},{7,3},{8,12},{9,13},{10,... | collective-permute-start | bytes 786440 | tf_op jit(solution)/shard_map/ppermute | solution.py:258
  112.7 1.5 %collective-permute-done.37 = bf16[1,32,2048]{2,1,0:T(8,128)(2,1)S(1)} collective-permute-done((bf16[1,32,2048]{2,1,0:T(8,128)(2,1)S(1)}, bf16[1,32,2048]{2,1,0:T(8,128)(2,1)S(1)}, u32[]{:S(2)}, u32[]{:S(2)}) %collective-permute-start.37) | collective-permute-done | bytes 131104 | tf_op jit(solution)/shard_map/ppermute | solution.py:258
  115.5 5.3 %collective-permute-done.40 = bf16[2,32,2048]{2,1,0:T(8,128)(2,1)S(1)} collective-permute-done((bf16[2,32,2048]{2,1,0:T(8,128)(2,1)S(1)}, bf16[2,32,2048]{2,1,0:T(8,128)(2,1)S(1)}, u32[]{:S(2)}, u32[]{:S(2)}) %collective-permute-start.40) | collective-permute-done | bytes 262176 | tf_op jit(solution)/shard_map/ppermute | solution.py:258
  121.1 1.6 %collective-permute-start.42 = (bf16[1,32,2048]{2,1,0:T(8,128)(2,1)S(1)}, bf16[1,32,2048]{2,1,0:T(8,128)(2,1)S(1)}, u32[]{:S(2)}, u32[]{:S(2)}) collective-permute-start(bf16[1,32,2048]{2,1,0:T(8,128)(2,1)S(1)} %slice.435), channel_id=1, source_target_pairs={{0,2},{1,3},{2,0},{3,1},{4,6},{5,7},{6,4},{7,5},{8,10},{9,11},{10,... | collective-permute-start | bytes 393224 | tf_op jit(solution)/shard_map/ppermute | solution.py:258
  123.4 2.7 %collective-permute-done.42 = bf16[1,32,2048]{2,1,0:T(8,128)(2,1)S(1)} collective-permute-done((bf16[1,32,2048]{2,1,0:T(8,128)(2,1)S(1)}, bf16[1,32,2048]{2,1,0:T(8,128)(2,1)S(1)}, u32[]{:S(2)}, u32[]{:S(2)}) %collective-permute-start.42) | collective-permute-done | bytes 131104 | tf_op jit(solution)/shard_map/ppermute | solution.py:258
  126.2 1.6 %collective-permute-done.41 = bf16[1,32,2048]{2,1,0:T(8,128)(2,1)S(1)} collective-permute-done((bf16[1,32,2048]{2,1,0:T(8,128)(2,1)S(1)}, bf16[1,32,2048]{2,1,0:T(8,128)(2,1)S(1)}, u32[]{:S(2)}, u32[]{:S(2)}) %collective-permute-start.41) | collective-permute-done | bytes 131104 | tf_op jit(solution)/shard_map/ppermute | solution.py:258
  127.9 12.4 %conditional.1 = (bf16[128,2048]{1,0:T(8,128)(2,1)S(1)}) conditional(s32[]{:T(128)} %clamp.3, bf16[128,2048]{1,0:T(8,128)(2,1)S(1)} %fusion.65, bf16[128,2048]{1,0:T(8,128)(2,1)S(1)} %fusion.65, bf16[128,2048]{1,0:T(8,128)(2,1)S(1)} %fusion.65, bf16[128,2048]{1,0:T(8,128)(2,1)S(1)} %fusion.65, ...), branch_computations={%region_8.10_spmd, %region_9.11_spmd, %region_10.12_spmd, %region_... | conditional | bytes 3145776 | solution.py:310
  128.0 3.5 %collective-permute-start.2 = (bf16[128,2048]{1,0:T(8,128)(2,1)S(1)}, bf16[128,2048]{1,0:T(8,128)(2,1)S(1)}, u32[]{:S(2)}, u32[]{:S(2)}) collective-permute-start(bf16[128,2048]{1,0:T(8,128)(2,1)S(1)} %param.5), channel_id=1, source_target_pairs={{0,0},{8,16},{16,24},{24,8},{1,1},{9,17},{17,25},{25,9},{2,2},{10,... | collective-permute-start | bytes 1572872 | tf_op jit(solution)/shard_map/cond/branch_3_fun/ppermute | solution.py:308
  131.5 8.8 %collective-permute-done.2 = bf16[128,2048]{1,0:T(8,128)(2,1)S(1)} collective-permute-done((bf16[128,2048]{1,0:T(8,128)(2,1)S(1)}, bf16[128,2048]{1,0:T(8,128)(2,1)S(1)}, u32[]{:S(2)}, u32[]{:S(2)}) %collective-permute-start.2) | collective-permute-done | bytes 524320 | tf_op jit(solution)/shard_map/cond/branch_3_fun/ppermute | solution.py:308
  (159 shorter events, 40.6 us)
Async XLA Ops:
  0.0 5.8 %copy-start.3 = (bf16[192,1024]{1,0:T(8,128)(2,1)S(1)}, bf16[192,1024]{1,0:T(8,128)(2,1)}, u32[]{:S(2)}) copy-start(bf16[192,1024]{1,0:T(8,128)(2,1)} %param.51) | copy-start | bytes 1179652
  6.0 5.4 %copy-start.5 = (s32[24,4]{0,1:T(4,128)S(1)}, s32[24,4]{0,1:T(4,128)}, u32[]{:S(2)}) copy-start(s32[24,4]{0,1:T(4,128)} %constant.76.clone) | copy-start | bytes 1156
  6.0 5.4 %copy-start.8 = (s32[4]{0:T(128)S(1)}, s32[4]{0:T(128)}, u32[]{:S(2)}) copy-start(s32[4]{0:T(128)} %param.53) | copy-start | bytes 52
  6.0 7.4 %copy-start.11 = (s32[4]{0:T(128)S(1)}, s32[4]{0:T(128)}, u32[]{:S(2)}) copy-start(s32[4]{0:T(128)} %param.52) | copy-start | bytes 52
  6.0 9.2 %copy-start.6 = (s32[8]{0:T(128)S(1)}, s32[8]{0:T(128)}, u32[]{:S(2)}) copy-start(s32[8]{0:T(128)} %constant.75.clone) | copy-start | bytes 100
  6.0 9.2 %copy-start.7 = (s32[8]{0:T(128)S(1)}, s32[8]{0:T(128)}, u32[]{:S(2)}) copy-start(s32[8]{0:T(128)} %constant.74.clone) | copy-start | bytes 100
  7.6 24.9 %all-to-all-start = ((bf16[8,774,128]{2,1,0:T(8,128)(2,1)}), bf16[8,774,128]{2,1,0:T(8,128)(2,1)S(1)}, u32[]{:S(2)}, u32[]{:S(2)}) async-start(bf16[8,774,128]{2,1,0:T(8,128)(2,1)} %copy.114), calls=%async_computation | async-start | bytes 3178496 | tf_op jit(solution)/shard_map/all_to_all | solution.py:71
  37.6 14.1 %copy-start.1 = (bf16[128,2048]{1,0:T(8,128)(2,1)S(1)}, bf16[128,2048]{1,0:T(8,128)(2,1)}, u32[]{:S(2)}) copy-start(bf16[128,2048]{1,0:T(8,128)(2,1)} %param.46) | copy-start | bytes 1572868
  40.7 14.1 %copy-start.4 = (f32[2048]{0:T(1024)S(1)}, f32[2048]{0:T(1024)}, u32[]{:S(2)}) copy-start(f32[2048]{0:T(1024)} %param.55) | copy-start | bytes 24580
  41.5 10.3 %all-to-all-start.1 = ((bf16[8,128,128]{1,2,0:T(8,128)(2,1)}), bf16[8,128,128]{1,2,0:T(8,128)(2,1)S(1)}, u32[]{:S(2)}, u32[]{:S(2)}) async-start(bf16[8,128,128]{1,2,0:T(8,128)(2,1)} %copy.119), calls=%async_computation.1 | async-start | bytes 524288 | tf_op jit(solution)/shard_map/all_to_all | solution.py:102
  55.0 5.0 %collective-permute-start.24 = (bf16[1,32,2048]{2,1,0:T(8,128)(2,1)S(1)}, bf16[1,32,2048]{2,1,0:T(8,128)(2,1)S(1)}, u32[]{:S(2)}, u32[]{:S(2)}) collective-permute-start(bf16[1,32,2048]{2,1,0:T(8,128)(2,1)S(1)} %get-tuple-element.136), channel_id=1, source_target_pairs={{0,2},{1,3},{2,0},{3,1},{4,6},{5,7},{6,4},{7,5},{8,10},{9,11},{10,... | collective-permute-start | bytes 393224 | tf_op jit(solution)/shard_map/ppermute | solution.py:258
  55.6 5.1 %collective-permute-start.23 = (bf16[1,32,2048]{2,1,0:T(8,128)(2,1)S(1)}, bf16[1,32,2048]{2,1,0:T(8,128)(2,1)S(1)}, u32[]{:S(2)}, u32[]{:S(2)}) collective-permute-start(bf16[1,32,2048]{2,1,0:T(8,128)(2,1)S(1)} %get-tuple-element.137), channel_id=1, source_target_pairs={{0,4},{1,5},{2,6},{3,7},{4,0},{5,1},{6,2},{7,3},{8,12},{9,13},{10,... | collective-permute-start | bytes 393224 | tf_op jit(solution)/shard_map/ppermute | solution.py:258
  60.8 7.0 %collective-permute-start.25 = (bf16[2,32,2048]{2,1,0:T(8,128)(2,1)S(1)}, bf16[2,32,2048]{2,1,0:T(8,128)(2,1)S(1)}, u32[]{:S(2)}, u32[]{:S(2)}) collective-permute-start(bf16[2,32,2048]{2,1,0:T(8,128)(2,1)S(1)} %pad_maximum_fusion.14), channel_id=1, source_target_pairs={{0,2},{1,3},{2,0},{3,1},{4,6},{5,7},{6,4},{7,5},{8,10},{9,11},{10,... | collective-permute-start | bytes 786440 | tf_op jit(solution)/shard_map/ppermute | solution.py:258
  63.5 6.4 %collective-permute-start.26 = (bf16[2,32,2048]{2,1,0:T(8,128)(2,1)S(1)}, bf16[2,32,2048]{2,1,0:T(8,128)(2,1)S(1)}, u32[]{:S(2)}, u32[]{:S(2)}) collective-permute-start(bf16[2,32,2048]{2,1,0:T(8,128)(2,1)S(1)} %pad_maximum_fusion.15), channel_id=1, source_target_pairs={{0,4},{1,5},{2,6},{3,7},{4,0},{5,1},{6,2},{7,3},{8,12},{9,13},{10,... | collective-permute-start | bytes 786440 | tf_op jit(solution)/shard_map/ppermute | solution.py:258
  71.1 2.9 %collective-permute-start.27 = (bf16[2,4,32,2048]{3,2,1,0:T(8,128)(2,1)}, bf16[2,4,32,2048]{3,2,1,0:T(8,128)(2,1)S(1)}, u32[]{:S(2)}, u32[]{:S(2)}) collective-permute-start(bf16[2,4,32,2048]{3,2,1,0:T(8,128)(2,1)} %pad_maximum_fusion.2), channel_id=1, source_target_pairs={{0,1},{1,0},{2,3},{3,2},{4,5},{5,4},{6,7},{7,6},{8,9},{9,8},{10,11... | collective-permute-start | bytes 3145736 | tf_op jit(solution)/shard_map/ppermute | solution.py:258
  71.3 2.9 %copy-start.9 = (bf16[2,2048,512]{2,1,0:T(8,128)(2,1)S(1)}, bf16[2,2048,512]{2,1,0:T(8,128)(2,1)}, u32[]{:S(2)}) copy-start(bf16[2,2048,512]{2,1,0:T(8,128)(2,1)} %param.58) | copy-start | bytes 12582916
  76.8 7.6 %collective-permute-start.29 = (bf16[1,32,2048]{2,1,0:T(8,128)(2,1)S(1)}, bf16[1,32,2048]{2,1,0:T(8,128)(2,1)S(1)}, u32[]{:S(2)}, u32[]{:S(2)}) collective-permute-start(bf16[1,32,2048]{2,1,0:T(8,128)(2,1)S(1)} %bitcast.223), channel_id=1, source_target_pairs={{0,2},{1,3},{2,0},{3,1},{4,6},{5,7},{6,4},{7,5},{8,10},{9,11},{10,... | collective-permute-start | bytes 393224 | tf_op jit(solution)/shard_map/ppermute | solution.py:258
  77.8 6.7 %collective-permute-start.28 = (bf16[1,32,2048]{2,1,0:T(8,128)(2,1)S(1)}, bf16[1,32,2048]{2,1,0:T(8,128)(2,1)S(1)}, u32[]{:S(2)}, u32[]{:S(2)}) collective-permute-start(bf16[1,32,2048]{2,1,0:T(8,128)(2,1)S(1)} %bitcast.221), channel_id=1, source_target_pairs={{0,4},{1,5},{2,6},{3,7},{4,0},{5,1},{6,2},{7,3},{8,12},{9,13},{10,... | collective-permute-start | bytes 393224 | tf_op jit(solution)/shard_map/ppermute | solution.py:258
  84.5 8.0 %collective-permute-start.30 = (bf16[2,32,2048]{2,1,0:T(8,128)(2,1)S(1)}, bf16[2,32,2048]{2,1,0:T(8,128)(2,1)S(1)}, u32[]{:S(2)}, u32[]{:S(2)}) collective-permute-start(bf16[2,32,2048]{2,1,0:T(8,128)(2,1)S(1)} %pad_maximum_fusion.16), channel_id=1, source_target_pairs={{0,2},{1,3},{2,0},{3,1},{4,6},{5,7},{6,4},{7,5},{8,10},{9,11},{10,... | collective-permute-start | bytes 786440 | tf_op jit(solution)/shard_map/ppermute | solution.py:258
  85.9 7.6 %collective-permute-start.31 = (bf16[2,32,2048]{2,1,0:T(8,128)(2,1)S(1)}, bf16[2,32,2048]{2,1,0:T(8,128)(2,1)S(1)}, u32[]{:S(2)}, u32[]{:S(2)}) collective-permute-start(bf16[2,32,2048]{2,1,0:T(8,128)(2,1)S(1)} %pad_maximum_fusion.17), channel_id=1, source_target_pairs={{0,4},{1,5},{2,6},{3,7},{4,0},{5,1},{6,2},{7,3},{8,12},{9,13},{10,... | collective-permute-start | bytes 786440 | tf_op jit(solution)/shard_map/ppermute | solution.py:258
  87.6 6.4 %collective-permute-start.33 = (bf16[2,4,32,2048]{3,2,1,0:T(8,128)(2,1)S(1)}, bf16[2,4,32,2048]{3,2,1,0:T(8,128)(2,1)S(1)}, u32[]{:S(2)}, u32[]{:S(2)}) collective-permute-start(bf16[2,4,32,2048]{3,2,1,0:T(8,128)(2,1)S(1)} %pad_maximum_fusion.8), channel_id=1, source_target_pairs={{0,1},{1,0},{2,3},{3,2},{4,5},{5,4},{6,7},{7,6},{8,9},{9,8},{10,11... | collective-permute-start | bytes 3145736 | tf_op jit(solution)/shard_map/ppermute | solution.py:258
  93.7 2.7 %collective-permute-start.32 = (bf16[2,4,32,2048]{3,2,1,0:T(8,128)(2,1)S(1)}, bf16[2,4,32,2048]{3,2,1,0:T(8,128)(2,1)S(1)}, u32[]{:S(2)}, u32[]{:S(2)}) collective-permute-start(bf16[2,4,32,2048]{3,2,1,0:T(8,128)(2,1)S(1)} %pad_maximum_fusion.5), channel_id=1, source_target_pairs={{0,1},{1,0},{2,3},{3,2},{4,5},{5,4},{6,7},{7,6},{8,9},{9,8},{10,11... | collective-permute-start | bytes 3145736 | tf_op jit(solution)/shard_map/ppermute | solution.py:258
  99.5 8.6 %collective-permute-start.35 = (bf16[2,32,2048]{2,1,0:T(8,128)(2,1)S(1)}, bf16[2,32,2048]{2,1,0:T(8,128)(2,1)S(1)}, u32[]{:S(2)}, u32[]{:S(2)}) collective-permute-start(bf16[2,32,2048]{2,1,0:T(8,128)(2,1)S(1)} %slice.433), channel_id=1, source_target_pairs={{0,4},{1,5},{2,6},{3,7},{4,0},{5,1},{6,2},{7,3},{8,12},{9,13},{10,... | collective-permute-start | bytes 786440 | tf_op jit(solution)/shard_map/ppermute | solution.py:258
  101.1 8.1 %collective-permute-start.34 = (bf16[2,32,2048]{2,1,0:T(8,128)(2,1)S(1)}, bf16[2,32,2048]{2,1,0:T(8,128)(2,1)S(1)}, u32[]{:S(2)}, u32[]{:S(2)}) collective-permute-start(bf16[2,32,2048]{2,1,0:T(8,128)(2,1)S(1)} %slice.434), channel_id=1, source_target_pairs={{0,2},{1,3},{2,0},{3,1},{4,6},{5,7},{6,4},{7,5},{8,10},{9,11},{10,... | collective-permute-start | bytes 786440 | tf_op jit(solution)/shard_map/ppermute | solution.py:258
  107.8 2.9 %collective-permute-start.38 = (bf16[2,4,32,2048]{3,2,1,0:T(8,128)(2,1)S(1)}, bf16[2,4,32,2048]{3,2,1,0:T(8,128)(2,1)S(1)}, u32[]{:S(2)}, u32[]{:S(2)}) collective-permute-start(bf16[2,4,32,2048]{3,2,1,0:T(8,128)(2,1)S(1)} %pad_maximum_fusion.9), channel_id=1, source_target_pairs={{0,1},{1,0},{2,3},{3,2},{4,5},{5,4},{6,7},{7,6},{8,9},{9,8},{10,11... | collective-permute-start | bytes 3145736 | tf_op jit(solution)/shard_map/ppermute | solution.py:258
  109.2 5.0 %collective-permute-start.37 = (bf16[1,32,2048]{2,1,0:T(8,128)(2,1)S(1)}, bf16[1,32,2048]{2,1,0:T(8,128)(2,1)S(1)}, u32[]{:S(2)}, u32[]{:S(2)}) collective-permute-start(bf16[1,32,2048]{2,1,0:T(8,128)(2,1)S(1)} %slice.437), channel_id=1, source_target_pairs={{0,2},{1,3},{2,0},{3,1},{4,6},{5,7},{6,4},{7,5},{8,10},{9,11},{10,... | collective-permute-start | bytes 393224 | tf_op jit(solution)/shard_map/ppermute | solution.py:258
  110.2 12.5 %collective-permute-start.36 = (bf16[1,32,2048]{2,1,0:T(8,128)(2,1)S(1)}, bf16[1,32,2048]{2,1,0:T(8,128)(2,1)S(1)}, u32[]{:S(2)}, u32[]{:S(2)}) collective-permute-start(bf16[1,32,2048]{2,1,0:T(8,128)(2,1)S(1)} %slice.438), channel_id=1, source_target_pairs={{0,4},{1,5},{2,6},{3,7},{4,0},{5,1},{6,2},{7,3},{8,12},{9,13},{10,... | collective-permute-start | bytes 393224 | tf_op jit(solution)/shard_map/ppermute | solution.py:258
  111.1 9.6 %collective-permute-start.40 = (bf16[2,32,2048]{2,1,0:T(8,128)(2,1)S(1)}, bf16[2,32,2048]{2,1,0:T(8,128)(2,1)S(1)}, u32[]{:S(2)}, u32[]{:S(2)}) collective-permute-start(bf16[2,32,2048]{2,1,0:T(8,128)(2,1)S(1)} %slice.431), channel_id=1, source_target_pairs={{0,4},{1,5},{2,6},{3,7},{4,0},{5,1},{6,2},{7,3},{8,12},{9,13},{10,... | collective-permute-start | bytes 786440 | tf_op jit(solution)/shard_map/ppermute | solution.py:258
  114.3 6.7 %collective-permute-start.39 = (bf16[2,32,2048]{2,1,0:T(8,128)(2,1)S(1)}, bf16[2,32,2048]{2,1,0:T(8,128)(2,1)S(1)}, u32[]{:S(2)}, u32[]{:S(2)}) collective-permute-start(bf16[2,32,2048]{2,1,0:T(8,128)(2,1)S(1)} %slice.432), channel_id=1, source_target_pairs={{0,2},{1,3},{2,0},{3,1},{4,6},{5,7},{6,4},{7,5},{8,10},{9,11},{10,... | collective-permute-start | bytes 786440 | tf_op jit(solution)/shard_map/ppermute | solution.py:258
  121.1 5.0 %collective-permute-start.42 = (bf16[1,32,2048]{2,1,0:T(8,128)(2,1)S(1)}, bf16[1,32,2048]{2,1,0:T(8,128)(2,1)S(1)}, u32[]{:S(2)}, u32[]{:S(2)}) collective-permute-start(bf16[1,32,2048]{2,1,0:T(8,128)(2,1)S(1)} %slice.435), channel_id=1, source_target_pairs={{0,2},{1,3},{2,0},{3,1},{4,6},{5,7},{6,4},{7,5},{8,10},{9,11},{10,... | collective-permute-start | bytes 393224 | tf_op jit(solution)/shard_map/ppermute | solution.py:258
  122.7 5.0 %collective-permute-start.41 = (bf16[1,32,2048]{2,1,0:T(8,128)(2,1)S(1)}, bf16[1,32,2048]{2,1,0:T(8,128)(2,1)S(1)}, u32[]{:S(2)}, u32[]{:S(2)}) collective-permute-start(bf16[1,32,2048]{2,1,0:T(8,128)(2,1)S(1)} %slice.436), channel_id=1, source_target_pairs={{0,4},{1,5},{2,6},{3,7},{4,0},{5,1},{6,2},{7,3},{8,12},{9,13},{10,... | collective-permute-start | bytes 393224 | tf_op jit(solution)/shard_map/ppermute | solution.py:258
  128.0 12.3 %collective-permute-start.2 = (bf16[128,2048]{1,0:T(8,128)(2,1)S(1)}, bf16[128,2048]{1,0:T(8,128)(2,1)S(1)}, u32[]{:S(2)}, u32[]{:S(2)}) collective-permute-start(bf16[128,2048]{1,0:T(8,128)(2,1)S(1)} %param.5), channel_id=1, source_target_pairs={{0,0},{8,16},{16,24},{24,8},{1,1},{9,17},{17,25},{25,9},{2,2},{10,... | collective-permute-start | bytes 1572872 | tf_op jit(solution)/shard_map/cond/branch_3_fun/ppermute | solution.py:308
  (3 other events, 5.6 us)

commit v3 on v2

--- a/solution.py
+++ b/solution.py
@@ -4,6 +4,8 @@
 import jax
 import jax.numpy as jnp
 from jax import lax
+from jax.experimental import pallas as pl
+from jax.experimental.pallas import tpu as pltpu
 from jax.sharding import PartitionSpec as P
 
 HEAD_DIM = 128
@@ -51,6 +53,31 @@
     )
 
 
+def pack_by_destination(sources, extra, width):
+    ctx_count = extra.shape[0]
+    counts = [x.shape[0] for x in sources] + [extra.shape[1]]
+    offsets = [sum(counts[:i]) for i in range(len(counts))]
+    total_rows = sum(counts)
+
+    def body(*refs):
+        out_ref = refs[-1]
+        for i, ref in enumerate(refs[:-2]):
+            out_ref[0, offsets[i] : offsets[i] + counts[i], :] = ref[...]
+        out_ref[0, offsets[-1] :, :] = refs[-2][0]
+
+    in_specs = [pl.BlockSpec((x.shape[0], width), lambda c: (0, c)) for x in sources]
+    in_specs.append(pl.BlockSpec((1, extra.shape[1], width), lambda c: (c, 0, 0)))
+    moved = 2 * total_rows * width * ctx_count * extra.dtype.itemsize
+    return pl.pallas_call(
+        body,
+        grid=(ctx_count,),
+        in_specs=in_specs,
+        out_specs=pl.BlockSpec((1, total_rows, width), lambda c: (c, 0, 0)),
+        out_shape=jax.ShapeDtypeStruct((ctx_count, total_rows, width), extra.dtype),
+        cost_estimate=pl.CostEstimate(flops=0, transcendentals=0, bytes_accessed=moved),
+    )(*sources, extra)
+
+
 def attend_by_head(queries, span_keys, span_values, cache_keys, cache_values, length, extra):
     token_count, column_count = queries.shape
     head_count = column_count // HEAD_DIM
@@ -62,11 +89,7 @@
     block_rows = token_count + cached_rows
     sources = [queries, span_keys, cache_keys, span_values, cache_values]
     base_rows = sum(x.shape[0] for x in sources)
-    packed = jnp.concatenate(
-        [x.reshape(x.shape[0], ctx_count, width).transpose(1, 0, 2) for x in sources]
-        + [extra],
-        1,
-    )
+    packed = pack_by_destination(sources, extra, width)
     packed_rows = packed.shape[1]
     got = lax.all_to_all(packed, "ctx", split_axis=0, concat_axis=0, tiled=True)
     got = got.reshape(ctx_count, packed_rows, local_heads, HEAD_DIM)

time: 144 us -> 147 us (1.021)
  the two profiles are of different devices: /device:TPU:16 before, /device:TPU:8 now
where the time goes in v3:
time: 147 us; the launch traced here: 148 us
  waiting for transfers between devices  74.6 us (51%)
  starting transfers between devices  25.7 us (17%)
  matrix products  23.8 us (16%)
  other arithmetic  10.5 us (7%)
  local copies, waits for them, and re-layouts  7 us (5%)
  Pallas kernels  5.23 us (4%)
    ppermute x20, waiting for transfers between devices, swap(): return lax.ppermute(rows, 'ctx', [(c, c ^ mask) for c in range(ctx_count)])  31.6 us
    ppermute x1, waiting for transfers between devices, mover(): return lambda rows: lax.ppermute(rows, 'req', pairs)  19.2 us
    all_to_all x1, waiting for transfers between devices, attend_by_head(): got = lax.all_to_all(packed, 'ctx', split_axis=0, concat_axis=0, tiled=True)  17.2 us
    ppermute x20, starting transfers between devices, swap(): return lax.ppermute(rows, 'ctx', [(c, c ^ mask) for c in range(ctx_count)])  16.8 us
    all_to_all x1, waiting for transfers between devices, attend_by_head(): lax.all_to_all(head_out, 'ctx', split_axis=0, concat_axis=0, tiled=True)  6.65 us
    dot_general x4, matrix products, experts_on(): up_val = jnp.dot(rows, up_proj[j], preferred_element_type=jnp.float32)  5.58 us
    dot_general x4, matrix products, experts_on(): jnp.dot(activated, down_proj[j], preferred_element_type=jnp.float32)  5.42 us
    pallas_call x1, Pallas kernels, pack_by_destination(): pl.pallas_call(body, grid=(ctx_count,), in_specs=in_specs, out_specs=pl.B...  5.23 us
  transfers between devices with their start and end apart: 23, of which 17 were waited for; matrix products, arithmetic and copies ran while one was open for 13% of the time, Pallas kernels for 0%

profile of v3, /device:TPU:8, one launch (start us, length us, event | category | flops | bytes accessed | tf_op | source)
XLA Modules:
  0.0 148.3 jit_solution(12581880715313969781)
XLA Ops:
  1.4 5.2 %shard_map.214 = bf16[8,774,128]{2,1,0:T(8,128)(2,1)} custom-call(bf16[128,1024]{1,0:T(8,128)(2,1)} %refs_0_.1, bf16[128,1024]{1,0:T(8,128)(2,1)} %refs_1_.1, bf16[192,1024]{1,0:T(8,128)(2,1)} %refs_2_.1, bf16[128,1024]{1,0:T(8,128)(2,1)} %refs_3_.1, bf16[192,1024]{1,0:T(8,128)(2,1)} %refs_4_.1, bf16[8,6,128]{2,1,0:T(8,128)(2,1)} %copy.78.refs_5_), custom_call_target="tpu_custom_call" | custom-call | bytes 3170304 | tf_op jit(solution)/shard_map/pallas_call | solution.py:71
  6.7 3.7 %all-to-all-start = ((bf16[8,774,128]{2,1,0:T(8,128)(2,1)}), bf16[8,774,128]{2,1,0:T(8,128)(2,1)S(1)}, u32[]{:S(2)}, u32[]{:S(2)}) async-start(bf16[8,774,128]{2,1,0:T(8,128)(2,1)} %shard_map.214), calls=%async_computation | async-start | bytes 3178496 | tf_op jit(solution)/shard_map/all_to_all | solution.py:94
  14.4 17.2 %all-to-all-done = bf16[8,774,128]{2,1,0:T(8,128)(2,1)S(1)} async-done(((bf16[8,774,128]{2,1,0:T(8,128)(2,1)}), bf16[8,774,128]{2,1,0:T(8,128)(2,1)S(1)}, u32[]{:S(2)}, u32[]{:S(2)}) %all-to-all-start) | async-done | bytes 1585184 | tf_op jit(solution)/shard_map/all_to_all | solution.py:94
  31.8 1.8 %fusion = (f32[1024]{0:T(1024)S(1)}, f32[1024,2560]{1,0:T(8,128)S(1)}) fusion(pred[2560]{0:T(1024)(128)(4,1)S(1)} %fusion.85, bf16[1024,128]{1,0:T(8,128)(2,1)S(1)} %bitcast.178, bf16[2560,128]{1,0:T(8,128)(2,1)S(1)} %bitcast.173), kind=kOutput, calls=%fused_computation.6 | convolution fusion | flops 678951936 | bytes 11409920 | tf_op jit(solution)/shard_map/thd,phd->htp/dot_general | solution.py:110
  33.6 2.7 %fusion.1 = f32[1024]{0:T(1024)S(1)} fusion(f32[1024,2560]{1,0:T(8,128)S(1)} %get-tuple-element.159, f32[1024]{0:T(1024)S(1)} %get-tuple-element.158, pred[2560]{0:T(1024)(128)(4,1)S(1)} %fusion.85), kind=kLoop, calls=%fused_computation.7 | loop fusion | flops 13106176 | bytes 10496512 | tf_op jit(solution)/shard_map/reduce_sum | solution.py:116
  36.3 3.0 %fusion.72 = bf16[16,8,8,128]{3,1,2,0:T(8,128)(2,1)S(1)} fusion(bf16[2560,128]{1,0:T(8,128)(2,1)S(1)} %bitcast.193, f32[1024,2560]{1,0:T(8,128)S(1)} %get-tuple-element.159, f32[1024]{0:T(1024)S(1)} %get-tuple-element.158, pred[2560]{0:T(1024)(128)(4,1)S(1)} %fusion.85, f32[1024]{0:T(1024)S(1)} %fusion.1), kind=kOutput, calls=%fused_computation.79 | convolution fusion | flops 684457984 | bytes 11414016 | tf_op jit(solution)/shard_map/htp,phd->thd/dot_general | solution.py:117
  40.1 3.6 %all-to-all-start.1 = ((bf16[8,128,128]{1,2,0:T(8,128)(2,1)}), bf16[8,128,128]{1,2,0:T(8,128)(2,1)S(1)}, u32[]{:S(2)}, u32[]{:S(2)}) async-start(bf16[8,128,128]{1,2,0:T(8,128)(2,1)} %copy.79), calls=%async_computation.1 | async-start | bytes 524288 | tf_op jit(solution)/shard_map/all_to_all | solution.py:125
  43.7 6.6 %all-to-all-done.1 = bf16[8,128,128]{1,2,0:T(8,128)(2,1)S(1)} async-done(((bf16[8,128,128]{1,2,0:T(8,128)(2,1)}), bf16[8,128,128]{1,2,0:T(8,128)(2,1)S(1)}, u32[]{:S(2)}, u32[]{:S(2)}) %all-to-all-start.1) | async-done | bytes 262176 | tf_op jit(solution)/shard_map/all_to_all | solution.py:125
  50.4 3.0 %multiply_reduce_fusion = (f32[128]{0:T(128)S(1)}, f32[128,2048]{1,0:T(8,128)S(1)}) fusion(bf16[128,1024]{0,1:T(8,128)(2,1)S(1)} %bitcast.181, bf16[1024,2048]{1,0:T(8,128)(2,1)} %param.54, bf16[128,2048]{1,0:T(8,128)(2,1)S(1)} %copy-done.1), kind=kOutput, calls=%fused_computation.76 | convolution fusion | flops 537919360 | bytes 6029824 | tf_op jit(solution)/shard_map/dot_general | solution.py:199
  54.9 3.8 %collective-permute-done.24 = bf16[1,32,2048]{2,1,0:T(8,128)(2,1)S(1)} collective-permute-done((bf16[1,32,2048]{2,1,0:T(8,128)(2,1)S(1)}, bf16[1,32,2048]{2,1,0:T(8,128)(2,1)S(1)}, u32[]{:S(2)}, u32[]{:S(2)}) %collective-permute-start.24) | collective-permute-done | bytes 131104 | tf_op jit(solution)/shard_map/ppermute | solution.py:281
  59.4 1.5 collective-permute-start.25
  64.1 2.3 %collective-permute-done.25 = bf16[2,32,2048]{2,1,0:T(8,128)(2,1)S(1)} collective-permute-done((bf16[2,32,2048]{2,1,0:T(8,128)(2,1)S(1)}, bf16[2,32,2048]{2,1,0:T(8,128)(2,1)S(1)}, u32[]{:S(2)}, u32[]{:S(2)}) %collective-permute-start.25) | collective-permute-done | bytes 262176 | tf_op jit(solution)/shard_map/ppermute | solution.py:281
  66.5 2.1 %collective-permute-done.26 = bf16[2,32,2048]{2,1,0:T(8,128)(2,1)S(1)} collective-permute-done((bf16[2,32,2048]{2,1,0:T(8,128)(2,1)S(1)}, bf16[2,32,2048]{2,1,0:T(8,128)(2,1)S(1)}, u32[]{:S(2)}, u32[]{:S(2)}) %collective-permute-start.26) | collective-permute-done | bytes 262176 | tf_op jit(solution)/shard_map/ppermute | solution.py:281
  70.0 2.6 %collective-permute-done.27 = bf16[2,4,32,2048]{3,2,1,0:T(8,128)(2,1)S(1)} collective-permute-done((bf16[2,4,32,2048]{3,2,1,0:T(8,128)(2,1)}, bf16[2,4,32,2048]{3,2,1,0:T(8,128)(2,1)S(1)}, u32[]{:S(2)}, u32[]{:S(2)}) %collective-permute-start.27) | collective-permute-done | bytes 1048608 | tf_op jit(solution)/shard_map/ppermute | solution.py:281
  78.1 1.4 fusion.59
  81.6 1.4 fusion.102
  83.1 1.3 collective-permute-start.30
  84.6 1.6 %collective-permute-start.31 = (bf16[2,32,2048]{2,1,0:T(8,128)(2,1)S(1)}, bf16[2,32,2048]{2,1,0:T(8,128)(2,1)S(1)}, u32[]{:S(2)}, u32[]{:S(2)}) collective-permute-start(bf16[2,32,2048]{2,1,0:T(8,128)(2,1)S(1)} %pad_maximum_fusion.17), channel_id=1, source_target_pairs={{0,4},{1,5},{2,6},{3,7},{4,0},{5,1},{6,2},{7,3},{8,12},{9,13},{10,... | collective-permute-start | bytes 786440 | tf_op jit(solution)/shard_map/ppermute | solution.py:281
  86.3 4.8 %collective-permute-done.30 = bf16[2,32,2048]{2,1,0:T(8,128)(2,1)S(1)} collective-permute-done((bf16[2,32,2048]{2,1,0:T(8,128)(2,1)S(1)}, bf16[2,32,2048]{2,1,0:T(8,128)(2,1)S(1)}, u32[]{:S(2)}, u32[]{:S(2)}) %collective-permute-start.30) | collective-permute-done | bytes 262176 | tf_op jit(solution)/shard_map/ppermute | solution.py:281
  92.9 2.1 %collective-permute-done.32 = bf16[2,4,32,2048]{3,2,1,0:T(8,128)(2,1)S(1)} collective-permute-done((bf16[2,4,32,2048]{3,2,1,0:T(8,128)(2,1)S(1)}, bf16[2,4,32,2048]{3,2,1,0:T(8,128)(2,1)S(1)}, u32[]{:S(2)}, u32[]{:S(2)}) %collective-permute-start.32) | collective-permute-done | bytes 1048608 | tf_op jit(solution)/shard_map/ppermute | solution.py:281
  98.1 1.6 %collective-permute-start.35 = (bf16[2,32,2048]{2,1,0:T(8,128)(2,1)S(1)}, bf16[2,32,2048]{2,1,0:T(8,128)(2,1)S(1)}, u32[]{:S(2)}, u32[]{:S(2)}) collective-permute-start(bf16[2,32,2048]{2,1,0:T(8,128)(2,1)S(1)} %slice.434), channel_id=1, source_target_pairs={{0,4},{1,5},{2,6},{3,7},{4,0},{5,1},{6,2},{7,3},{8,12},{9,13},{10,... | collective-permute-start | bytes 786440 | tf_op jit(solution)/shard_map/ppermute | solution.py:281
  101.9 1.6 %fusion.56 = bf16[512,512]{1,0:T(8,128)(2,1)S(1)} fusion(bf16[512,2048]{1,0:T(8,128)(2,1)S(1)} %pad_maximum_fusion, bf16[2,2048,512]{2,1,0:T(8,128)(2,1)S(1)} %copy-done.9, f32[512,512]{1,0:T(8,128)S(1)} %fusion.22), kind=kOutput, calls=%fused_computation.58 | convolution fusion | flops 1075314688 | bytes 5767168 | tf_op jit(solution)/shard_map/dot_general | solution.py:209
  104.8 1.4 fusion.103
  109.7 1.6 %collective-permute-start.40 = (bf16[2,32,2048]{2,1,0:T(8,128)(2,1)S(1)}, bf16[2,32,2048]{2,1,0:T(8,128)(2,1)S(1)}, u32[]{:S(2)}, u32[]{:S(2)}) collective-permute-start(bf16[2,32,2048]{2,1,0:T(8,128)(2,1)S(1)} %slice.432), channel_id=1, source_target_pairs={{0,4},{1,5},{2,6},{3,7},{4,0},{5,1},{6,2},{7,3},{8,12},{9,13},{10,... | collective-permute-start | bytes 786440 | tf_op jit(solution)/shard_map/ppermute | solution.py:281
  111.3 1.5 %collective-permute-done.37 = bf16[1,32,2048]{2,1,0:T(8,128)(2,1)S(1)} collective-permute-done((bf16[1,32,2048]{2,1,0:T(8,128)(2,1)S(1)}, bf16[1,32,2048]{2,1,0:T(8,128)(2,1)S(1)}, u32[]{:S(2)}, u32[]{:S(2)}) %collective-permute-start.37) | collective-permute-done | bytes 131104 | tf_op jit(solution)/shard_map/ppermute | solution.py:281
  114.1 5.3 %collective-permute-done.40 = bf16[2,32,2048]{2,1,0:T(8,128)(2,1)S(1)} collective-permute-done((bf16[2,32,2048]{2,1,0:T(8,128)(2,1)S(1)}, bf16[2,32,2048]{2,1,0:T(8,128)(2,1)S(1)}, u32[]{:S(2)}, u32[]{:S(2)}) %collective-permute-start.40) | collective-permute-done | bytes 262176 | tf_op jit(solution)/shard_map/ppermute | solution.py:281
  119.7 1.6 %collective-permute-start.42 = (bf16[1,32,2048]{2,1,0:T(8,128)(2,1)S(1)}, bf16[1,32,2048]{2,1,0:T(8,128)(2,1)S(1)}, u32[]{:S(2)}, u32[]{:S(2)}) collective-permute-start(bf16[1,32,2048]{2,1,0:T(8,128)(2,1)S(1)} %slice.436), channel_id=1, source_target_pairs={{0,2},{1,3},{2,0},{3,1},{4,6},{5,7},{6,4},{7,5},{8,10},{9,11},{10,... | collective-permute-start | bytes 393224 | tf_op jit(solution)/shard_map/ppermute | solution.py:281
  122.0 2.7 %collective-permute-done.42 = bf16[1,32,2048]{2,1,0:T(8,128)(2,1)S(1)} collective-permute-done((bf16[1,32,2048]{2,1,0:T(8,128)(2,1)S(1)}, bf16[1,32,2048]{2,1,0:T(8,128)(2,1)S(1)}, u32[]{:S(2)}, u32[]{:S(2)}) %collective-permute-start.42) | collective-permute-done | bytes 131104 | tf_op jit(solution)/shard_map/ppermute | solution.py:281
  124.8 1.6 %collective-permute-done.41 = bf16[1,32,2048]{2,1,0:T(8,128)(2,1)S(1)} collective-permute-done((bf16[1,32,2048]{2,1,0:T(8,128)(2,1)S(1)}, bf16[1,32,2048]{2,1,0:T(8,128)(2,1)S(1)}, u32[]{:S(2)}, u32[]{:S(2)}) %collective-permute-start.41) | collective-permute-done | bytes 131104 | tf_op jit(solution)/shard_map/ppermute | solution.py:281
  126.6 20.9 %conditional.1 = (bf16[128,2048]{1,0:T(8,128)(2,1)S(1)}) conditional(s32[]{:T(128)} %clamp.3, bf16[128,2048]{1,0:T(8,128)(2,1)S(1)} %fusion.65, bf16[128,2048]{1,0:T(8,128)(2,1)S(1)} %fusion.65, bf16[128,2048]{1,0:T(8,128)(2,1)S(1)} %fusion.65, bf16[128,2048]{1,0:T(8,128)(2,1)S(1)} %fusion.65, ...), branch_computations={%region_8.10_spmd, %region_9.11_spmd, %region_10.12_spmd, %region_... | conditional | bytes 3145776 | solution.py:333
  126.7 1.6 %collective-permute-start.21 = (bf16[128,2048]{1,0:T(8,128)(2,1)S(1)}, bf16[128,2048]{1,0:T(8,128)(2,1)S(1)}, u32[]{:S(2)}, u32[]{:S(2)}) collective-permute-start(bf16[128,2048]{1,0:T(8,128)(2,1)S(1)} %param.24), channel_id=1, source_target_pairs={{0,24},{8,16},{16,0},{24,8},{1,25},{9,17},{17,1},{25,9},{2,26},{10... | collective-permute-start | bytes 1572872 | tf_op jit(solution)/shard_map/cond/branch_22_fun/ppermute | solution.py:331
  128.3 19.2 %collective-permute-done.21 = bf16[128,2048]{1,0:T(8,128)(2,1)S(1)} collective-permute-done((bf16[128,2048]{1,0:T(8,128)(2,1)S(1)}, bf16[128,2048]{1,0:T(8,128)(2,1)S(1)}, u32[]{:S(2)}, u32[]{:S(2)}) %collective-permute-start.21) | collective-permute-done | bytes 524320 | tf_op jit(solution)/shard_map/cond/branch_22_fun/ppermute | solution.py:331
  (140 shorter events, 35.5 us)
Async XLA Ops:
  0.0 10.4 %copy-start.4 = (s32[24,4]{0,1:T(4,128)S(1)}, s32[24,4]{0,1:T(4,128)}, u32[]{:S(2)}) copy-start(s32[24,4]{0,1:T(4,128)} %constant.76.clone) | copy-start | bytes 1156
  0.0 14.4 %copy-start.5 = (s32[8]{0:T(128)S(1)}, s32[8]{0:T(128)}, u32[]{:S(2)}) copy-start(s32[8]{0:T(128)} %constant.75.clone) | copy-start | bytes 100
  0.0 14.4 %copy-start.6 = (s32[8]{0:T(128)S(1)}, s32[8]{0:T(128)}, u32[]{:S(2)}) copy-start(s32[8]{0:T(128)} %constant.74.clone) | copy-start | bytes 100
  0.0 10.4 %copy-start.7 = (s32[4]{0:T(128)S(1)}, s32[4]{0:T(128)}, u32[]{:S(2)}) copy-start(s32[4]{0:T(128)} %param.53) | copy-start | bytes 52
  0.0 12.4 %copy-start.10 = (s32[4]{0:T(128)S(1)}, s32[4]{0:T(128)}, u32[]{:S(2)}) copy-start(s32[4]{0:T(128)} %param.52) | copy-start | bytes 52
  6.7 24.9 %all-to-all-start = ((bf16[8,774,128]{2,1,0:T(8,128)(2,1)}), bf16[8,774,128]{2,1,0:T(8,128)(2,1)S(1)}, u32[]{:S(2)}, u32[]{:S(2)}) async-start(bf16[8,774,128]{2,1,0:T(8,128)(2,1)} %shard_map.214), calls=%async_computation | async-start | bytes 3178496 | tf_op jit(solution)/shard_map/all_to_all | solution.py:94
  36.3 14.1 %copy-start.1 = (bf16[128,2048]{1,0:T(8,128)(2,1)S(1)}, bf16[128,2048]{1,0:T(8,128)(2,1)}, u32[]{:S(2)}) copy-start(bf16[128,2048]{1,0:T(8,128)(2,1)} %param.46) | copy-start | bytes 1572868
  39.3 14.1 %copy-start.3 = (f32[2048]{0:T(1024)S(1)}, f32[2048]{0:T(1024)}, u32[]{:S(2)}) copy-start(f32[2048]{0:T(1024)} %param.55) | copy-start | bytes 24580
  40.1 10.3 %all-to-all-start.1 = ((bf16[8,128,128]{1,2,0:T(8,128)(2,1)}), bf16[8,128,128]{1,2,0:T(8,128)(2,1)S(1)}, u32[]{:S(2)}, u32[]{:S(2)}) async-start(bf16[8,128,128]{1,2,0:T(8,128)(2,1)} %copy.79), calls=%async_computation.1 | async-start | bytes 524288 | tf_op jit(solution)/shard_map/all_to_all | solution.py:125
  53.6 5.0 %collective-permute-start.24 = (bf16[1,32,2048]{2,1,0:T(8,128)(2,1)S(1)}, bf16[1,32,2048]{2,1,0:T(8,128)(2,1)S(1)}, u32[]{:S(2)}, u32[]{:S(2)}) collective-permute-start(bf16[1,32,2048]{2,1,0:T(8,128)(2,1)S(1)} %get-tuple-element.136), channel_id=1, source_target_pairs={{0,2},{1,3},{2,0},{3,1},{4,6},{5,7},{6,4},{7,5},{8,10},{9,11},{10,... | collective-permute-start | bytes 393224 | tf_op jit(solution)/shard_map/ppermute | solution.py:281
  54.2 5.1 %collective-permute-start.23 = (bf16[1,32,2048]{2,1,0:T(8,128)(2,1)S(1)}, bf16[1,32,2048]{2,1,0:T(8,128)(2,1)S(1)}, u32[]{:S(2)}, u32[]{:S(2)}) collective-permute-start(bf16[1,32,2048]{2,1,0:T(8,128)(2,1)S(1)} %get-tuple-element.137), channel_id=1, source_target_pairs={{0,4},{1,5},{2,6},{3,7},{4,0},{5,1},{6,2},{7,3},{8,12},{9,13},{10,... | collective-permute-start | bytes 393224 | tf_op jit(solution)/shard_map/ppermute | solution.py:281
  59.4 7.0 %collective-permute-start.25 = (bf16[2,32,2048]{2,1,0:T(8,128)(2,1)S(1)}, bf16[2,32,2048]{2,1,0:T(8,128)(2,1)S(1)}, u32[]{:S(2)}, u32[]{:S(2)}) collective-permute-start(bf16[2,32,2048]{2,1,0:T(8,128)(2,1)S(1)} %pad_maximum_fusion.14), channel_id=1, source_target_pairs={{0,2},{1,3},{2,0},{3,1},{4,6},{5,7},{6,4},{7,5},{8,10},{9,11},{10,... | collective-permute-start | bytes 786440 | tf_op jit(solution)/shard_map/ppermute | solution.py:281
  62.1 6.4 %collective-permute-start.26 = (bf16[2,32,2048]{2,1,0:T(8,128)(2,1)S(1)}, bf16[2,32,2048]{2,1,0:T(8,128)(2,1)S(1)}, u32[]{:S(2)}, u32[]{:S(2)}) collective-permute-start(bf16[2,32,2048]{2,1,0:T(8,128)(2,1)S(1)} %pad_maximum_fusion.15), channel_id=1, source_target_pairs={{0,4},{1,5},{2,6},{3,7},{4,0},{5,1},{6,2},{7,3},{8,12},{9,13},{10,... | collective-permute-start | bytes 786440 | tf_op jit(solution)/shard_map/ppermute | solution.py:281
  69.7 2.9 %collective-permute-start.27 = (bf16[2,4,32,2048]{3,2,1,0:T(8,128)(2,1)}, bf16[2,4,32,2048]{3,2,1,0:T(8,128)(2,1)S(1)}, u32[]{:S(2)}, u32[]{:S(2)}) collective-permute-start(bf16[2,4,32,2048]{3,2,1,0:T(8,128)(2,1)} %pad_maximum_fusion.2), channel_id=1, source_target_pairs={{0,1},{1,0},{2,3},{3,2},{4,5},{5,4},{6,7},{7,6},{8,9},{9,8},{10,11... | collective-permute-start | bytes 3145736 | tf_op jit(solution)/shard_map/ppermute | solution.py:281
  69.9 2.9 %copy-start.8 = (bf16[2,2048,512]{2,1,0:T(8,128)(2,1)S(1)}, bf16[2,2048,512]{2,1,0:T(8,128)(2,1)}, u32[]{:S(2)}) copy-start(bf16[2,2048,512]{2,1,0:T(8,128)(2,1)} %param.58) | copy-start | bytes 12582916
  74.1 2.6 %copy-start.9 = (bf16[2,2048,512]{2,1,0:T(8,128)(2,1)S(1)}, bf16[2,2048,512]{2,1,0:T(8,128)(2,1)}, u32[]{:S(2)}) copy-start(bf16[2,2048,512]{2,1,0:T(8,128)(2,1)} %param.59) | copy-start | bytes 12582916
  75.4 7.6 %collective-permute-start.29 = (bf16[1,32,2048]{2,1,0:T(8,128)(2,1)S(1)}, bf16[1,32,2048]{2,1,0:T(8,128)(2,1)S(1)}, u32[]{:S(2)}, u32[]{:S(2)}) collective-permute-start(bf16[1,32,2048]{2,1,0:T(8,128)(2,1)S(1)} %bitcast.196), channel_id=1, source_target_pairs={{0,2},{1,3},{2,0},{3,1},{4,6},{5,7},{6,4},{7,5},{8,10},{9,11},{10,... | collective-permute-start | bytes 393224 | tf_op jit(solution)/shard_map/ppermute | solution.py:281
  76.4 6.7 %collective-permute-start.28 = (bf16[1,32,2048]{2,1,0:T(8,128)(2,1)S(1)}, bf16[1,32,2048]{2,1,0:T(8,128)(2,1)S(1)}, u32[]{:S(2)}, u32[]{:S(2)}) collective-permute-start(bf16[1,32,2048]{2,1,0:T(8,128)(2,1)S(1)} %bitcast.194), channel_id=1, source_target_pairs={{0,4},{1,5},{2,6},{3,7},{4,0},{5,1},{6,2},{7,3},{8,12},{9,13},{10,... | collective-permute-start | bytes 393224 | tf_op jit(solution)/shard_map/ppermute | solution.py:281
  83.1 8.0 %collective-permute-start.30 = (bf16[2,32,2048]{2,1,0:T(8,128)(2,1)S(1)}, bf16[2,32,2048]{2,1,0:T(8,128)(2,1)S(1)}, u32[]{:S(2)}, u32[]{:S(2)}) collective-permute-start(bf16[2,32,2048]{2,1,0:T(8,128)(2,1)S(1)} %pad_maximum_fusion.16), channel_id=1, source_target_pairs={{0,2},{1,3},{2,0},{3,1},{4,6},{5,7},{6,4},{7,5},{8,10},{9,11},{10,... | collective-permute-start | bytes 786440 | tf_op jit(solution)/shard_map/ppermute | solution.py:281
  84.6 7.6 %collective-permute-start.31 = (bf16[2,32,2048]{2,1,0:T(8,128)(2,1)S(1)}, bf16[2,32,2048]{2,1,0:T(8,128)(2,1)S(1)}, u32[]{:S(2)}, u32[]{:S(2)}) collective-permute-start(bf16[2,32,2048]{2,1,0:T(8,128)(2,1)S(1)} %pad_maximum_fusion.17), channel_id=1, source_target_pairs={{0,4},{1,5},{2,6},{3,7},{4,0},{5,1},{6,2},{7,3},{8,12},{9,13},{10,... | collective-permute-start | bytes 786440 | tf_op jit(solution)/shard_map/ppermute | solution.py:281
  86.2 6.4 %collective-permute-start.33 = (bf16[2,4,32,2048]{3,2,1,0:T(8,128)(2,1)S(1)}, bf16[2,4,32,2048]{3,2,1,0:T(8,128)(2,1)S(1)}, u32[]{:S(2)}, u32[]{:S(2)}) collective-permute-start(bf16[2,4,32,2048]{3,2,1,0:T(8,128)(2,1)S(1)} %pad_maximum_fusion.8), channel_id=1, source_target_pairs={{0,1},{1,0},{2,3},{3,2},{4,5},{5,4},{6,7},{7,6},{8,9},{9,8},{10,11... | collective-permute-start | bytes 3145736 | tf_op jit(solution)/shard_map/ppermute | solution.py:281
  92.3 2.7 %collective-permute-start.32 = (bf16[2,4,32,2048]{3,2,1,0:T(8,128)(2,1)S(1)}, bf16[2,4,32,2048]{3,2,1,0:T(8,128)(2,1)S(1)}, u32[]{:S(2)}, u32[]{:S(2)}) collective-permute-start(bf16[2,4,32,2048]{3,2,1,0:T(8,128)(2,1)S(1)} %pad_maximum_fusion.5), channel_id=1, source_target_pairs={{0,1},{1,0},{2,3},{3,2},{4,5},{5,4},{6,7},{7,6},{8,9},{9,8},{10,11... | collective-permute-start | bytes 3145736 | tf_op jit(solution)/shard_map/ppermute | solution.py:281
  98.1 8.6 %collective-permute-start.35 = (bf16[2,32,2048]{2,1,0:T(8,128)(2,1)S(1)}, bf16[2,32,2048]{2,1,0:T(8,128)(2,1)S(1)}, u32[]{:S(2)}, u32[]{:S(2)}) collective-permute-start(bf16[2,32,2048]{2,1,0:T(8,128)(2,1)S(1)} %slice.434), channel_id=1, source_target_pairs={{0,4},{1,5},{2,6},{3,7},{4,0},{5,1},{6,2},{7,3},{8,12},{9,13},{10,... | collective-permute-start | bytes 786440 | tf_op jit(solution)/shard_map/ppermute | solution.py:281
  99.7 8.1 %collective-permute-start.34 = (bf16[2,32,2048]{2,1,0:T(8,128)(2,1)S(1)}, bf16[2,32,2048]{2,1,0:T(8,128)(2,1)S(1)}, u32[]{:S(2)}, u32[]{:S(2)}) collective-permute-start(bf16[2,32,2048]{2,1,0:T(8,128)(2,1)S(1)} %slice.435), channel_id=1, source_target_pairs={{0,2},{1,3},{2,0},{3,1},{4,6},{5,7},{6,4},{7,5},{8,10},{9,11},{10,... | collective-permute-start | bytes 786440 | tf_op jit(solution)/shard_map/ppermute | solution.py:281
  106.4 2.9 %collective-permute-start.38 = (bf16[2,4,32,2048]{3,2,1,0:T(8,128)(2,1)S(1)}, bf16[2,4,32,2048]{3,2,1,0:T(8,128)(2,1)S(1)}, u32[]{:S(2)}, u32[]{:S(2)}) collective-permute-start(bf16[2,4,32,2048]{3,2,1,0:T(8,128)(2,1)S(1)} %pad_maximum_fusion.9), channel_id=1, source_target_pairs={{0,1},{1,0},{2,3},{3,2},{4,5},{5,4},{6,7},{7,6},{8,9},{9,8},{10,11... | collective-permute-start | bytes 3145736 | tf_op jit(solution)/shard_map/ppermute | solution.py:281
  107.8 5.0 %collective-permute-start.37 = (bf16[1,32,2048]{2,1,0:T(8,128)(2,1)S(1)}, bf16[1,32,2048]{2,1,0:T(8,128)(2,1)S(1)}, u32[]{:S(2)}, u32[]{:S(2)}) collective-permute-start(bf16[1,32,2048]{2,1,0:T(8,128)(2,1)S(1)} %slice.438), channel_id=1, source_target_pairs={{0,2},{1,3},{2,0},{3,1},{4,6},{5,7},{6,4},{7,5},{8,10},{9,11},{10,... | collective-permute-start | bytes 393224 | tf_op jit(solution)/shard_map/ppermute | solution.py:281
  108.8 12.5 %collective-permute-start.36 = (bf16[1,32,2048]{2,1,0:T(8,128)(2,1)S(1)}, bf16[1,32,2048]{2,1,0:T(8,128)(2,1)S(1)}, u32[]{:S(2)}, u32[]{:S(2)}) collective-permute-start(bf16[1,32,2048]{2,1,0:T(8,128)(2,1)S(1)} %slice.439), channel_id=1, source_target_pairs={{0,4},{1,5},{2,6},{3,7},{4,0},{5,1},{6,2},{7,3},{8,12},{9,13},{10,... | collective-permute-start | bytes 393224 | tf_op jit(solution)/shard_map/ppermute | solution.py:281
  109.7 9.7 %collective-permute-start.40 = (bf16[2,32,2048]{2,1,0:T(8,128)(2,1)S(1)}, bf16[2,32,2048]{2,1,0:T(8,128)(2,1)S(1)}, u32[]{:S(2)}, u32[]{:S(2)}) collective-permute-start(bf16[2,32,2048]{2,1,0:T(8,128)(2,1)S(1)} %slice.432), channel_id=1, source_target_pairs={{0,4},{1,5},{2,6},{3,7},{4,0},{5,1},{6,2},{7,3},{8,12},{9,13},{10,... | collective-permute-start | bytes 786440 | tf_op jit(solution)/shard_map/ppermute | solution.py:281
  112.9 6.7 %collective-permute-start.39 = (bf16[2,32,2048]{2,1,0:T(8,128)(2,1)S(1)}, bf16[2,32,2048]{2,1,0:T(8,128)(2,1)S(1)}, u32[]{:S(2)}, u32[]{:S(2)}) collective-permute-start(bf16[2,32,2048]{2,1,0:T(8,128)(2,1)S(1)} %slice.433), channel_id=1, source_target_pairs={{0,2},{1,3},{2,0},{3,1},{4,6},{5,7},{6,4},{7,5},{8,10},{9,11},{10,... | collective-permute-start | bytes 786440 | tf_op jit(solution)/shard_map/ppermute | solution.py:281
  119.7 5.0 %collective-permute-start.42 = (bf16[1,32,2048]{2,1,0:T(8,128)(2,1)S(1)}, bf16[1,32,2048]{2,1,0:T(8,128)(2,1)S(1)}, u32[]{:S(2)}, u32[]{:S(2)}) collective-permute-start(bf16[1,32,2048]{2,1,0:T(8,128)(2,1)S(1)} %slice.436), channel_id=1, source_target_pairs={{0,2},{1,3},{2,0},{3,1},{4,6},{5,7},{6,4},{7,5},{8,10},{9,11},{10,... | collective-permute-start | bytes 393224 | tf_op jit(solution)/shard_map/ppermute | solution.py:281
  121.4 5.0 %collective-permute-start.41 = (bf16[1,32,2048]{2,1,0:T(8,128)(2,1)S(1)}, bf16[1,32,2048]{2,1,0:T(8,128)(2,1)S(1)}, u32[]{:S(2)}, u32[]{:S(2)}) collective-permute-start(bf16[1,32,2048]{2,1,0:T(8,128)(2,1)S(1)} %slice.437), channel_id=1, source_target_pairs={{0,4},{1,5},{2,6},{3,7},{4,0},{5,1},{6,2},{7,3},{8,12},{9,13},{10,... | collective-permute-start | bytes 393224 | tf_op jit(solution)/shard_map/ppermute | solution.py:281
  126.7 20.8 %collective-permute-start.21 = (bf16[128,2048]{1,0:T(8,128)(2,1)S(1)}, bf16[128,2048]{1,0:T(8,128)(2,1)S(1)}, u32[]{:S(2)}, u32[]{:S(2)}) collective-permute-start(bf16[128,2048]{1,0:T(8,128)(2,1)S(1)} %param.24), channel_id=1, source_target_pairs={{0,24},{8,16},{16,0},{24,8},{1,25},{9,17},{17,1},{25,9},{2,26},{10... | collective-permute-start | bytes 1572872 | tf_op jit(solution)/shard_map/cond/branch_22_fun/ppermute | solution.py:331
  (2 other events, 3.0 us)
